TPU v7x, 128 devices: a whole 4x4x4 slice. The times are simulated.
128 devices in a mesh: chan: 16 (over y_lo, z, core), band: 8 (over x, y_hi).
Axes of the slice: x: 4, y: 4 (y_hi: 2, y_lo: 2; y = y_hi * 2 + y_lo), z: 4, core: 2. Of those that a mesh axis runs over, the one named last changes fastest.
Arguments:
- raw: bfloat16 [128, 2560, 2747], P(('chan', 'band')), may hold values from -600 to 600
- offsets: int32 [128], P(('chan', 'band')), may hold values from 0 to 127
- taps: bfloat16 [63], replicated, may hold values from -0.75 to 0.75
- partner: int32 [2, 16], replicated, may hold values from 0 to 15, as said below
Outputs:
- cross: float32 [2, 2, 128, 2560, 160], P(None, None, 'band', 'chan')
Inputs may be any that keep to these rules, and one draw needn't show every extreme that they name: For each round r there is one number M of 1 to 15 with partner[r, a] = a xor M for every block a; the two rounds' numbers differ.
All inputs are finite; a program needn't handle non-finite values.
Results may differ from a plain program's by a relative error of at most 0.0041.
Values may be sent and summed in bfloat16 or wider, within the bound.
No kernel may reach another device: no remote copies, remote signals or barrier semaphores. Data moves between devices by JAX's collectives and lax.ppermute only.
A program may use at most 128 MiB of HBM per device.

v0:
```python
import math

import jax
import jax.numpy as jnp
from jax import lax
from jax.sharding import PartitionSpec as P

DEC = 10
TAPS = 63
W = 256
NF = 128
HALF = 32


def mean_matrix(length, half):
    rows = jnp.arange(length, dtype=jnp.int32)[:, None]
    cols = jnp.arange(length, dtype=jnp.int32)[None, :]
    begins = jnp.clip(cols - half, 0, length - 2 * half - 1)
    inside = (rows >= begins) & (rows <= begins + 2 * half)
    return inside.astype(jnp.float32)


def dft_table(length, bins):
    samples = jnp.arange(length, dtype=jnp.int32)[:, None]
    freqs = jnp.arange(bins, dtype=jnp.int32)[None, :]
    phase = samples * freqs % length
    angle = phase.astype(jnp.float32) * (2.0 * math.pi / length)
    return jnp.concatenate([jnp.cos(angle), -jnp.sin(angle)], axis=1)


def filter_table(taps, phases):
    padded = jnp.pad(taps, (0, phases * DEC - TAPS))
    grid = padded.reshape(phases, DEC)
    rows = jnp.arange(W + phases - 1, dtype=jnp.int32)[:, None]
    cols = jnp.arange(W, dtype=jnp.int32)[None, :]
    onehot = (
        (rows - cols)[None, :, :] == jnp.arange(phases, dtype=jnp.int32)[:, None, None]
    ).astype(jnp.bfloat16)
    table = jnp.einsum("jqn,jr->qrn", onehot, grid, preferred_element_type=jnp.float32)
    return table.reshape((W + phases - 1) * DEC, W).astype(jnp.bfloat16)


def window_spectrum(segment, offset, table, level_matrix, transform):
    span = table.shape[0]
    piece = lax.dynamic_slice_in_dim(segment, offset, span, 1)
    decimated = jnp.dot(piece, table, preferred_element_type=jnp.float32)
    level = jnp.dot(jnp.abs(decimated), level_matrix, precision=lax.Precision.HIGHEST) / (
        2 * HALF + 1
    )
    normed = decimated / (level + 1e-05)
    spectrum = lax.dot_general(
        transform, normed, (((0,), (1,)), ((), ())), precision=lax.Precision.HIGHEST
    )
    return spectrum.reshape(2, NF, segment.shape[0]).astype(jnp.bfloat16)


def body(raw, offsets, taps, partner):
    phases = (TAPS + DEC - 1) // DEC
    table = filter_table(taps, phases)
    level_matrix = mean_matrix(W, HALF)
    transform = dft_table(W, NF)
    spectra = jnp.stack([window_spectrum(raw[0], offsets[0], table, level_matrix, transform)])
    chan_count = lax.axis_size("chan")
    band_count = lax.axis_size("band")
    window_count, part_count, bin_count, channel_count = spectra.shape
    arranged = spectra.reshape(
        window_count,
        part_count,
        band_count,
        bin_count // band_count,
        chan_count,
        channel_count // chan_count,
    )
    arranged = arranged.transpose(4, 2, 0, 1, 3, 5).reshape(
        chan_count * band_count * window_count,
        part_count,
        bin_count // band_count,
        channel_count // chan_count,
    )
    local = lax.all_to_all(arranged, ("chan", "band"), split_axis=0, concat_axis=0, tiled=True)
    width = local.shape[3]
    block = lax.axis_index("chan")
    block_count = partner.shape[1]
    own_partner = jnp.sum(
        jnp.where(jnp.arange(block_count, dtype=jnp.int32)[None, :] == block, partner, 0), axis=1
    )
    blank = jnp.zeros_like(local)
    carry = (blank, blank)
    piece = lax.all_gather(local, "chan", axis=3, tiled=True)
    span = piece.shape[3]
    chosen = []
    for round_index in range(2):
        placed = own_partner[round_index] * width
        inside = (placed >= 0) & (placed < span)
        window_rows = lax.dynamic_slice_in_dim(piece, jnp.clip(placed, 0, span - width), width, 3)
        chosen.append(jnp.where(inside, window_rows, carry[round_index]))
    first_other = chosen[0]
    second_other = chosen[1]
    factor = 1.0 / (W * math.sqrt(local.shape[0]))

    def stack_pair(other_rows):
        product = jnp.einsum(
            "wpfi,wqfj->fpqij", local, other_rows, preferred_element_type=jnp.float32
        )
        real_part = product[:, 0, 0] + product[:, 1, 1]
        imag_part = product[:, 1, 0] - product[:, 0, 1]
        return jnp.stack([real_part, imag_part]) * factor

    return jnp.stack([stack_pair(first_other), stack_pair(second_other)])


def solution(mesh):
    return jax.shard_map(
        body,
        mesh=mesh,
        in_specs=(P(("chan", "band"), None, None), P(("chan", "band")), P(), P()),
        out_specs=P(None, None, "band", "chan", None),
        check_vma=False,
    )
```

profile of v0, /device:TPU:2, one launch (start us, length us, event | category | flops | bytes accessed | tf_op | source)
XLA Modules:
  0.0 216.8 jit_solution(3624640159972781501)
XLA Ops:
  6.5 0.0 all-gather.2.cloned.1.call-start
  6.6 1.2 sine_negate_fusion
  8.5 0.7 pad.4
  9.1 0.1 reshape.230
  9.2 0.8 convert_bitcast_fusion
  10.0 0.5 convert_element_type.34
  10.5 7.2 %fusion = f32[2560,256]{1,0:T(8,128)S(1)} fusion(bf16[2620,256]{1,0:T(8,128)(2,1)S(1)} %convert_element_type.34, bf16[1,2560,2747]{1,2,0:T(8,128)(2,1)} %param.4, s32[]{:T(128)S(6)} %select_n.35), kind=kOutput, calls=%fused_computation | convolution fusion | flops 3434086400 | bytes 17397764 | tf_op jit(solution)/shard_map/dot_general | solution.py:46
  17.7 0.0 copy-start.1
  17.7 0.0 copy-start.2
  17.7 1.5 fusion.4
  19.2 0.0 copy-done.1
  19.2 0.0 copy-done.2
  19.2 4.4 %convolution_convert_fusion = bf16[256,2560]{1,0:T(8,128)(2,1)S(1)} fusion(f32[2560,256]{1,0:T(8,128)S(1)} %fusion.4, f32[256,128]{1,0:T(8,128)S(1)} %copy-done.1, f32[256,128]{1,0:T(8,128)S(1)} %copy-done.2), kind=kOutput, calls=%fused_computation.8 | convolution fusion | flops 2013986816 | bytes 4194304 | tf_op jit(solution)/shard_map/dot_general | solution.py:51
  23.6 2.6 %convert_element_type.36 = bf16[1,2,8,16,16,160]{5,4,3,2,1,0:T(8,128)(2,1)S(1)} reshape(bf16[256,2560]{1,0:T(8,128)(2,1)S(1)} %convolution_convert_fusion) | data formatting | bytes 2621440 | tf_op jit(solution)/shard_map/convert_element_type | solution.py:54
  26.2 0.7 copy.16
  26.9 2.4 %copy.17 = bf16[128,2,16,160]{3,1,2,0:T(2,128)(2,1)S(1)} copy(bf16[128,2,16,160]{3,2,1,0:T(8,128)(2,1)S(1)} %bitcast.54) | data formatting | bytes 2621440 | tf_op jit(solution)/shard_map/reshape | solution.py:74
  29.4 39.1 %all_to_all.5 = bf16[128,2,16,160]{3,1,2,0:T(2,128)(2,1)S(1)} all-to-all(bf16[128,2,16,160]{3,1,2,0:T(2,128)(2,1)S(1)} %copy.17), channel_id=1, replica_groups=mesh['chan'=16,'band'=8] {'chan','band'}, dimensions={0} | all-to-all | bytes 2621440 | tf_op jit(solution)/shard_map/all_to_all | solution.py:80
  68.5 0.0 copy-start.3
  68.5 3.8 %copy.18 = bf16[128,2,16,160]{0,3,1,2:T(8,128)(2,1)} copy(bf16[128,2,16,160]{3,1,2,0:T(2,128)(2,1)S(1)} %all_to_all.5) | data formatting | bytes 2621440 | tf_op jit(solution)/shard_map/all_to_all | solution.py:80
  72.3 0.0 all-gather.2.cloned.1.call-update
  72.4 0.0 copy-done.3
  72.4 0.1 select_reduce_fusion
  72.5 0.7 fusion.39
  74.5 106.7 %all-gather.2.cloned.1.call-done = bf16[128,2,16,2560]{0,3,1,2:T(8,128)(2,1)} async-done(((bf16[128,2,16,160]{0,3,1,2:T(8,128)(2,1)}), bf16[128,2,16,2560]{0,3,1,2:T(8,128)(2,1)}) %all-gather.2.cloned.1.call-update) | async-done | bytes 20971536 | tf_op jit(solution)/shard_map/all_gather | solution.py:89
  181.2 3.0 %convolution_bitcast_fusion.1 = f32[16,2,2,160,160]{3,4,1,2,0:T(8,128)S(1)} fusion(bf16[128,2,16,160,1]{3,1,2,0,4:T(2,128)(2,1)S(1)} %bitcast.52, bf16[128,2,16,2560]{0,3,1,2:T(8,128)(2,1)} %all-gather.2.cloned.1.call-done, s32[]{:T(128)} %bitcast.6, pred[]{:T(512)} %bitcast), kind=kOutput, calls=%fused_computation.11 | convolution fusion | flops 420085760 | bytes 9176064 | tf_op jit(solution)/shard_map/wpfi,wqfj->fpqij/dot_general | solution.py:102
  184.3 0.4 fusion.7
  184.7 0.4 fusion.9
  185.0 3.0 %convolution_bitcast_fusion = f32[16,2,2,160,160]{3,4,0,2,1:T(8,128)S(1)} fusion(bf16[128,2,16,160,1]{3,1,2,0,4:T(2,128)(2,1)S(1)} %bitcast.53, bf16[128,2,16,2560]{0,3,1,2:T(8,128)(2,1)} %all-gather.2.cloned.1.call-done, s32[]{:T(128)} %bitcast.14, pred[]{:T(512)} %bitcast.13), kind=kOutput, calls=%fused_computation.10 | convolution fusion | flops 420085760 | bytes 9176064 | tf_op jit(solution)/shard_map/wpfi,wqfj->fpqij/dot_general | solution.py:102
  188.1 2.3 %fusion.6 = (f32[1,1,16,160,160]{3,4,2,1,0:T(8,128)S(1)}, f32[1,1,16,160,160]{3,4,2,1,0:T(8,128)}) fusion(f32[16,2,2,160,160]{3,4,0,2,1:T(8,128)S(1)} %convolution_bitcast_fusion), kind=kLoop, calls=%fused_computation.15 | loop fusion | flops 819200 | bytes 9830400 | tf_op jit(solution)/shard_map/stack | solution.py:107
  190.4 0.0 copy-start
  190.4 0.8 maximum_multiply_fusion
  191.3 0.9 copy-done
  192.2 0.8 maximum_multiply_fusion.1
  193.0 4.8 %pad_maximum_fusion = f32[2,2,16,160,160]{3,4,2,1,0:T(8,128)} fusion(f32[1,2,16,160,160]{3,4,2,1,0:T(8,128)S(1)} %maximum_multiply_fusion.1, f32[1,2,16,160,160]{3,4,2,1,0:T(8,128)S(1)} %maximum_multiply_fusion), kind=kLoop, calls=%fused_computation.3 | loop fusion | flops 1638400 | bytes 13107200 | tf_op jit(solution)/shard_map/stack | solution.py:109
  197.8 12.1 %copy.24 = f32[2,2,16,160,160]{4,3,2,1,0:T(8,128)} copy(f32[2,2,16,160,160]{3,4,2,1,0:T(8,128)} %pad_maximum_fusion) | data formatting | bytes 13107200 | tf_op jit(solution)/shard_map/stack | solution.py:109
  (3 shorter events, 0.0 us)
Async XLA Ops:
  6.5 174.7 %all-gather.2.cloned.1.call-start = ((), (), s32[]{:S(2)}) async-start(), calls=%async_computation.1 | async-start | bytes 22282240 | tf_op jit(solution)/shard_map/all_gather | solution.py:89
  17.7 1.5 copy-start.1
  17.7 1.5 copy-start.2
  68.5 3.9 %copy-start.3 = (s32[2,16]{1,0:T(2,128)S(1)}, s32[2,16]{1,0:T(2,128)}, u32[]{:S(2)}) copy-start(s32[2,16]{1,0:T(2,128)} %param.7) | copy-start | bytes 388
  190.4 1.7 copy-start
Sparse Core Ops, SparseCore 0:
  72.5 108.7 all-gather.1
where the time goes:
time: 218 us; the launch traced here: 217 us
  waiting for transfers between devices  107 us (49%)
  blocking collectives  39.1 us (18%)
  local copies, waits for them, and re-layouts  24.4 us (11%)
  matrix products  19.9 us (9%)
  between operations  15.5 us (7%)
  other arithmetic  11 us (5%)
    all_gather x1, waiting for transfers between devices, body(): piece = lax.all_gather(local, 'chan', axis=3, tiled=True)  107 us
    all_to_all x1, blocking collectives, body(): lax.all_to_all(arranged, ('chan', 'band'), split_axis=0, concat_axis=0, t...  39.1 us
    another operation x1, local copies, waits for them, and re-layouts, body(): return jnp.stack([stack_pair(first_other), stack_pair(second_other)])  12.1 us
    dot_general x1, matrix products, window_spectrum(): decimated = jnp.dot(piece, table, preferred_element_type=jnp.float32)  7.16 us
    dot_general x2, matrix products, stack_pair(): jnp.einsum('wpfi,wqfj->fpqij', local, other_rows, preferred_element_type=...  6.07 us
    another operation x1, other arithmetic, body(): return jnp.stack([stack_pair(first_other), stack_pair(second_other)])  4.8 us
    dot_general x1, matrix products, window_spectrum(): lax.dot_general(transform, normed, (((0,), (1,)), ((), ())), precision=la...  4.41 us
  transfers between devices with their start and end apart: 1, of which 1 were waited for; matrix products, arithmetic and copies ran while one was open for 0% of the time, Pallas kernels for 0%

commit v1 on v0

--- a/solution.py
+++ b/solution.py
@@ -79,23 +79,18 @@
     )
     local = lax.all_to_all(arranged, ("chan", "band"), split_axis=0, concat_axis=0, tiled=True)
     width = local.shape[3]
-    block = lax.axis_index("chan")
-    block_count = partner.shape[1]
-    own_partner = jnp.sum(
-        jnp.where(jnp.arange(block_count, dtype=jnp.int32)[None, :] == block, partner, 0), axis=1
-    )
-    blank = jnp.zeros_like(local)
-    carry = (blank, blank)
-    piece = lax.all_gather(local, "chan", axis=3, tiled=True)
-    span = piece.shape[3]
-    chosen = []
-    for round_index in range(2):
-        placed = own_partner[round_index] * width
-        inside = (placed >= 0) & (placed < span)
-        window_rows = lax.dynamic_slice_in_dim(piece, jnp.clip(placed, 0, span - width), width, 3)
-        chosen.append(jnp.where(inside, window_rows, carry[round_index]))
-    first_other = chosen[0]
-    second_other = chosen[1]
+    chan_count_static = chan_count
+
+    def exchange(rows, number):
+        def branch(shift):
+            pairs = [(a, a ^ shift) for a in range(chan_count_static)]
+            return lambda x: lax.ppermute(x, "chan", pairs)
+
+        branches = [branch(shift) for shift in range(1, chan_count_static)]
+        return lax.switch(number - 1, branches, rows)
+
+    first_other = exchange(local, partner[0, 0])
+    second_other = exchange(local, partner[1, 0])
     factor = 1.0 / (W * math.sqrt(local.shape[0]))
 
     def stack_pair(other_rows):

time: 218 us -> 160 us (0.73)
  blocking collectives: 39.1 us -> 0 us
  waiting for transfers between devices: 107 us -> 89.4 us
  between operations: 15.5 us -> 2.04 us
  starting transfers between devices: 0.01 us -> 11.2 us
    all_gather x1 -> x0, waiting for transfers between devices: 107 us -> none  [body(): piece = lax.all_gather(local, 'chan', axis=3, tiled=True)]
    ppermute x0 -> x2, waiting for transfers between devices: none -> 62.3 us  [branch(): return lambda x: lax.ppermute(x, 'chan', pairs)]
    all_to_all x1 -> x0, blocking collectives: 39.1 us -> none  [body(): lax.all_to_all(arranged, ('chan', 'band'), split_axis=0, concat_axis=0, t...]
    all_to_all x0 -> x1, waiting for transfers between devices: none -> 27 us  [body(): lax.all_to_all(arranged, ('chan', 'band'), split_axis=0, concat_axis=0, t...]
    all_to_all x0 -> x1, starting transfers between devices: none -> 10.5 us  [body(): lax.all_to_all(arranged, ('chan', 'band'), split_axis=0, concat_axis=0, t...]
  transfers between devices with their start and end apart: 1 -> 3, of which waited for: 1 -> 3; matrix products, arithmetic and copies ran while one was open for 0% -> 0% of each run, Pallas kernels for 0% -> 0%
where the time goes in v1:
time: 160 us; the launch traced here: 159 us
  waiting for transfers between devices  89.4 us (56%)
  local copies, waits for them, and re-layouts  24.7 us (15%)
  matrix products  19.8 us (12%)
  other arithmetic  12.1 us (8%)
  starting transfers between devices  11.2 us (7%)
  between operations  2.04 us (1%)
    ppermute x2, waiting for transfers between devices, branch(): return lambda x: lax.ppermute(x, 'chan', pairs)  62.3 us
    all_to_all x1, waiting for transfers between devices, body(): lax.all_to_all(arranged, ('chan', 'band'), split_axis=0, concat_axis=0, t...  27 us
    another operation x1, local copies, waits for them, and re-layouts, body(): return jnp.stack([stack_pair(first_other), stack_pair(second_other)])  12.1 us
    all_to_all x1, starting transfers between devices, body(): lax.all_to_all(arranged, ('chan', 'band'), split_axis=0, concat_axis=0, t...  10.5 us
    dot_general x1, matrix products, window_spectrum(): decimated = jnp.dot(piece, table, preferred_element_type=jnp.float32)  7.15 us
    dot_general x2, matrix products, stack_pair(): jnp.einsum('wpfi,wqfj->fpqij', local, other_rows, preferred_element_type=...  5.95 us
    another operation x1, other arithmetic, body(): return jnp.stack([stack_pair(first_other), stack_pair(second_other)])  4.85 us
    another operation x3, other arithmetic, stack_pair(): return jnp.stack([real_part, imag_part]) * factor  4.65 us
  transfers between devices with their start and end apart: 3, of which 3 were waited for; matrix products, arithmetic and copies ran while one was open for 0% of the time, Pallas kernels for 0%

profile of v1, /device:TPU:2, one launch (start us, length us, event | category | flops | bytes accessed | tf_op | source)
XLA Modules:
  0.0 159.3 jit_solution(2775397458031531835)
XLA Ops:
  0.0 1.2 sine_negate_fusion
  1.3 0.7 pad.4
  1.9 0.1 reshape.213
  2.0 0.8 convert_bitcast_fusion
  2.8 0.5 convert_element_type.34
  4.0 7.1 %fusion = f32[2560,256]{1,0:T(8,128)S(1)} fusion(bf16[2620,256]{1,0:T(8,128)(2,1)S(1)} %convert_element_type.34, bf16[1,2560,2747]{1,2,0:T(8,128)(2,1)} %param.34, s32[]{:T(128)S(6)} %select_n.13), kind=kOutput, calls=%fused_computation | convolution fusion | flops 3434086400 | bytes 17397764 | tf_op jit(solution)/shard_map/dot_general | solution.py:46
  11.1 0.0 copy-start.2
  11.1 0.0 copy-start.3
  11.1 1.5 fusion.4
  12.6 0.0 copy-done.2
  12.6 0.0 copy-done.3
  12.6 4.4 %convolution_convert_fusion = bf16[256,2560]{1,0:T(8,128)(2,1)S(1)} fusion(f32[2560,256]{1,0:T(8,128)S(1)} %fusion.4, f32[256,128]{1,0:T(8,128)S(1)} %copy-done.2, f32[256,128]{1,0:T(8,128)S(1)} %copy-done.3), kind=kOutput, calls=%fused_computation.8 | convolution fusion | flops 2013986816 | bytes 4194304 | tf_op jit(solution)/shard_map/dot_general | solution.py:51
  17.1 2.6 %convert_element_type.36 = bf16[1,2,8,16,16,160]{5,4,3,2,1,0:T(8,128)(2,1)S(1)} reshape(bf16[256,2560]{1,0:T(8,128)(2,1)S(1)} %convolution_convert_fusion) | data formatting | bytes 2621440 | tf_op jit(solution)/shard_map/convert_element_type | solution.py:54
  19.7 0.7 copy.80
  20.4 3.7 %copy.81 = bf16[128,2,16,160]{3,1,2,0:T(2,128)(2,1)} copy(bf16[128,2,16,160]{3,2,1,0:T(8,128)(2,1)S(1)} %bitcast.50) | data formatting | bytes 2621440 | tf_op jit(solution)/shard_map/reshape | solution.py:74
  24.1 0.0 copy-start.4
  24.1 10.5 %all-to-all-start = ((bf16[128,2,16,160]{3,1,2,0:T(2,128)(2,1)}), bf16[128,2,16,160]{3,1,2,0:T(2,128)(2,1)S(1)}, u32[]{:S(2)}, u32[]{:S(2)}) async-start(bf16[128,2,16,160]{3,1,2,0:T(2,128)(2,1)} %copy.81), calls=%async_computation | async-start | bytes 4194304 | tf_op jit(solution)/shard_map/all_to_all | solution.py:80
  34.7 0.0 copy-done.4
  34.7 0.6 fusion.33
  36.4 27.0 %all-to-all-done = bf16[128,2,16,160]{3,1,2,0:T(2,128)(2,1)S(1)} async-done(((bf16[128,2,16,160]{3,1,2,0:T(2,128)(2,1)}), bf16[128,2,16,160]{3,1,2,0:T(2,128)(2,1)S(1)}, u32[]{:S(2)}, u32[]{:S(2)}) %all-to-all-start) | async-done | bytes 1310752 | tf_op jit(solution)/shard_map/all_to_all | solution.py:80
  63.5 2.1 %copy.82 = bf16[128,2,16,160]{0,3,2,1:T(8,128)(2,1)S(1)} copy(bf16[128,2,16,160]{3,1,2,0:T(2,128)(2,1)S(1)} %all-to-all-done) | data formatting | bytes 2621440 | tf_op jit(solution)/shard_map/all_to_all | solution.py:80
  65.6 31.0 %conditional.2 = (bf16[128,2,16,160]{0,3,2,1:T(8,128)(2,1)}) conditional(s32[]{:T(128)} %bitcast, bf16[128,2,16,160]{0,3,2,1:T(8,128)(2,1)S(1)} %copy.82, bf16[128,2,16,160]{0,3,2,1:T(8,128)(2,1)S(1)} %copy.82, bf16[128,2,16,160]{0,3,2,1:T(8,128)(2,1)S(1)} %copy.82, bf16[128,2,16,160]{0,3,2,1:T(8,128)(2,1)S(1)} %copy.82, ...), branch_computations={%region_0.1_spmd, %region_1.2_spmd, %region_2.3_spmd, %region_3.4_... | conditional | bytes 5242928 | solution.py:90
  65.6 0.1 collective-permute-start.8
  65.7 30.8 %collective-permute-done.8 = bf16[128,2,16,160]{0,3,2,1:T(8,128)(2,1)} collective-permute-done((bf16[128,2,16,160]{0,3,2,1:T(8,128)(2,1)S(1)}, bf16[128,2,16,160]{0,3,2,1:T(8,128)(2,1)}, u32[]{:S(2)}, u32[]{:S(2)}) %collective-permute-start.8) | collective-permute-done | bytes 1310752 | tf_op jit(solution)/shard_map/cond/branch_8_fun/ppermute | solution.py:87
  96.5 3.0 %convolution_bitcast_fusion.1 = f32[16,2,2,160,160]{3,4,1,2,0:T(8,128)S(1)} fusion(bf16[128,2,16,160,1]{3,1,2,0,4:T(2,128)(2,1)S(1)} %bitcast.48, bf16[128,2,16,160]{0,3,2,1:T(8,128)(2,1)} %get-tuple-element.75), kind=kOutput, calls=%fused_computation.11 | convolution fusion | flops 419430400 | bytes 9175040 | tf_op jit(solution)/shard_map/wpfi,wqfj->fpqij/dot_general | solution.py:97
  99.5 1.9 %fusion.7 = f32[1,1,16,160,160]{3,4,2,1,0:T(8,128)} fusion(f32[16,2,2,160,160]{3,4,1,2,0:T(8,128)S(1)} %convolution_bitcast_fusion.1), kind=kLoop, calls=%fused_computation.17 | loop fusion | flops 409600 | bytes 4915200 | tf_op jit(solution)/shard_map/stack | solution.py:102
  101.4 1.9 %fusion.9 = f32[1,1,16,160,160]{3,4,2,1,0:T(8,128)} fusion(f32[16,2,2,160,160]{3,4,1,2,0:T(8,128)S(1)} %convolution_bitcast_fusion.1), kind=kLoop, calls=%fused_computation.20 | loop fusion | flops 409600 | bytes 4915200 | tf_op jit(solution)/shard_map/stack | solution.py:102
  103.3 32.1 %conditional.3 = (bf16[128,2,16,160]{0,3,2,1:T(8,128)(2,1)}) conditional(s32[]{:T(128)} %bitcast.11, bf16[128,2,16,160]{0,3,2,1:T(8,128)(2,1)S(1)} %copy.82, bf16[128,2,16,160]{0,3,2,1:T(8,128)(2,1)S(1)} %copy.82, bf16[128,2,16,160]{0,3,2,1:T(8,128)(2,1)S(1)} %copy.82, ...), branch_computations={%region_15.16_spmd, %region_16.17_spmd, %region_17.18_spmd, %regio... | conditional | bytes 5242928 | solution.py:90
  103.3 0.6 collective-permute-start.18
  103.8 31.5 %collective-permute-done.18 = bf16[128,2,16,160]{0,3,2,1:T(8,128)(2,1)} collective-permute-done((bf16[128,2,16,160]{0,3,2,1:T(8,128)(2,1)S(1)}, bf16[128,2,16,160]{0,3,2,1:T(8,128)(2,1)}, u32[]{:S(2)}, u32[]{:S(2)}) %collective-permute-start.18) | collective-permute-done | bytes 1310752 | tf_op jit(solution)/shard_map/cond/branch_3_fun/ppermute | solution.py:87
  135.3 3.0 %convolution_bitcast_fusion = f32[16,2,2,160,160]{3,4,0,2,1:T(8,128)S(1)} fusion(bf16[128,2,16,160,1]{3,1,2,0,4:T(2,128)(2,1)S(1)} %bitcast.49, bf16[128,2,16,160]{0,3,2,1:T(8,128)(2,1)} %get-tuple-element.76), kind=kOutput, calls=%fused_computation.10 | convolution fusion | flops 419430400 | bytes 9175040 | tf_op jit(solution)/shard_map/wpfi,wqfj->fpqij/dot_general | solution.py:97
  138.3 0.9 fusion.6
  139.2 0.0 copy-start
  139.2 0.0 copy-start.1
  139.3 0.8 maximum_multiply_fusion.1
  140.1 0.9 copy-done
  141.0 0.8 copy-done.1
  141.8 0.5 maximum_multiply_fusion
  142.3 4.8 %pad_maximum_fusion = f32[2,2,16,160,160]{3,4,2,1,0:T(8,128)} fusion(f32[1,2,16,160,160]{3,4,2,1,0:T(8,128)S(1)} %maximum_multiply_fusion.1, f32[1,2,16,160,160]{3,4,2,1,0:T(8,128)S(1)} %maximum_multiply_fusion), kind=kLoop, calls=%fused_computation.3 | loop fusion | flops 1638400 | bytes 13107200 | tf_op jit(solution)/shard_map/stack | solution.py:104
  147.2 12.1 %copy.119 = f32[2,2,16,160,160]{4,3,2,1,0:T(8,128)} copy(f32[2,2,16,160,160]{3,4,2,1,0:T(8,128)} %pad_maximum_fusion) | data formatting | bytes 13107200 | tf_op jit(solution)/shard_map/stack | solution.py:104
  (2 shorter events, 0.0 us)
Async XLA Ops:
  11.1 1.5 copy-start.2
  11.1 1.5 copy-start.3
  24.1 10.5 %copy-start.4 = (s32[2,16]{1,0:T(2,128)S(1)}, s32[2,16]{1,0:T(2,128)}, u32[]{:S(2)}) copy-start(s32[2,16]{1,0:T(2,128)} %param.37) | copy-start | bytes 388
  24.1 39.3 %all-to-all-start = ((bf16[128,2,16,160]{3,1,2,0:T(2,128)(2,1)}), bf16[128,2,16,160]{3,1,2,0:T(2,128)(2,1)S(1)}, u32[]{:S(2)}, u32[]{:S(2)}) async-start(bf16[128,2,16,160]{3,1,2,0:T(2,128)(2,1)} %copy.81), calls=%async_computation | async-start | bytes 4194304 | tf_op jit(solution)/shard_map/all_to_all | solution.py:80
  65.6 30.9 %collective-permute-start.8 = (bf16[128,2,16,160]{0,3,2,1:T(8,128)(2,1)S(1)}, bf16[128,2,16,160]{0,3,2,1:T(8,128)(2,1)}, u32[]{:S(2)}, u32[]{:S(2)}) collective-permute-start(bf16[128,2,16,160]{0,3,2,1:T(8,128)(2,1)S(1)} %param.8), channel_id=1, source_target_pairs={{0,72},{8,64},{16,88},{24,80},{32,104},{40,96},{48,120},{56,112},{... | collective-permute-start | bytes 3932168 | tf_op jit(solution)/shard_map/cond/branch_8_fun/ppermute | solution.py:87
  103.3 32.1 %collective-permute-start.18 = (bf16[128,2,16,160]{0,3,2,1:T(8,128)(2,1)S(1)}, bf16[128,2,16,160]{0,3,2,1:T(8,128)(2,1)}, u32[]{:S(2)}, u32[]{:S(2)}) collective-permute-start(bf16[128,2,16,160]{0,3,2,1:T(8,128)(2,1)S(1)} %param.18), channel_id=1, source_target_pairs={{0,32},{8,40},{16,48},{24,56},{32,0},{40,8},{48,16},{56,24},{64,96... | collective-permute-start | bytes 3932168 | tf_op jit(solution)/shard_map/cond/branch_3_fun/ppermute | solution.py:87
  139.2 1.7 %copy-start = (f32[1,1,16,160,160]{3,4,2,1,0:T(8,128)S(1)}, f32[1,1,16,160,160]{3,4,2,1,0:T(8,128)}, u32[]{:S(2)}) copy-start(f32[1,1,16,160,160]{3,4,2,1,0:T(8,128)} %fusion.7) | copy-start | bytes 4915204
  139.2 2.5 %copy-start.1 = (f32[1,1,16,160,160]{3,4,2,1,0:T(8,128)S(1)}, f32[1,1,16,160,160]{3,4,2,1,0:T(8,128)}, u32[]{:S(2)}) copy-start(f32[1,1,16,160,160]{3,4,2,1,0:T(8,128)} %fusion.9) | copy-start | bytes 4915204

commit v2 on v1

--- a/solution.py
+++ b/solution.py
@@ -92,16 +92,19 @@
     first_other = exchange(local, partner[0, 0])
     second_other = exchange(local, partner[1, 0])
     factor = 1.0 / (W * math.sqrt(local.shape[0]))
-
-    def stack_pair(other_rows):
-        product = jnp.einsum(
-            "wpfi,wqfj->fpqij", local, other_rows, preferred_element_type=jnp.float32
-        )
-        real_part = product[:, 0, 0] + product[:, 1, 1]
-        imag_part = product[:, 1, 0] - product[:, 0, 1]
-        return jnp.stack([real_part, imag_part]) * factor
-
-    return jnp.stack([stack_pair(first_other), stack_pair(second_other)])
+    windows, parts, bins, width = local.shape
+    columns = []
+    for other_rows in (first_other, second_other):
+        real_rows = other_rows[:, 0]
+        imag_rows = other_rows[:, 1]
+        columns.append(other_rows)
+        columns.append(jnp.stack([-imag_rows, real_rows], axis=1))
+    mixed = jnp.stack(columns, axis=3).reshape(windows * parts, bins, len(columns), width)
+    own = local.reshape(windows * parts, bins, width)
+    own = jnp.broadcast_to(own[None], (len(columns),) + own.shape)
+    mixed = jnp.moveaxis(mixed, 2, 0)
+    product = jnp.einsum("qkfi,qkfj->qfij", own, mixed, preferred_element_type=jnp.float32)
+    return (product * factor).reshape(2, 2, bins, width, width)
 
 
 def solution(mesh):

time: 160 us -> 172 us (1.075)
  local copies, waits for them, and re-layouts: 24.7 us -> 41.4 us
  other arithmetic: 12.1 us -> 5.46 us
    another operation x4 -> x2, other arithmetic: 9.5 us -> 0.24 us  [body(): columns.append(jnp.stack([-imag_rows, real_rows], axis=1))]
    cond x0 -> x2, local copies, waits for them, and re-layouts: none -> 8.87 us  [exchange(): return lax.switch(number - 1, branches, rows)]
    another operation x1 -> x6, local copies, waits for them, and re-layouts: 12.1 us -> 20.5 us  [the longest x4 14.7 us: body(): jnp.stack(columns, axis=3)]
    neg x0 -> x2, other arithmetic: none -> 3.96 us  [body(): columns.append(jnp.stack([-imag_rows, real_rows], axis=1))]
    reshape x1 -> x0, local copies, waits for them, and re-layouts: 3.73 us -> none  [body(): arranged.transpose(4, 2, 0, 1, 3, 5)]
    broadcast_in_dim x0 -> x1, local copies, waits for them, and re-layouts: none -> 2.78 us  [body(): own = jnp.broadcast_to(own[None], (len(columns),) + own.shape)]
    dot_general x2 -> x1, matrix products: 5.95 us -> 6.77 us  [body(): jnp.einsum('qkfi,qkfj->qfij', own, mixed, preferred_element_type=jnp.floa...]
where the time goes in v2:
time: 172 us; the launch traced here: 170 us
  waiting for transfers between devices  87.8 us (51%)
  local copies, waits for them, and re-layouts  41.4 us (24%)
  matrix products  20.6 us (12%)
  starting transfers between devices  12.2 us (7%)
  other arithmetic  5.46 us (3%)
  between operations  1.97 us (1%)
    ppermute x2, waiting for transfers between devices, branch(): return lambda x: lax.ppermute(x, 'chan', pairs)  60.8 us
    all_to_all x1, waiting for transfers between devices, body(): lax.all_to_all(arranged, ('chan', 'band'), split_axis=0, concat_axis=0, t...  27 us
    another operation x4, local copies, waits for them, and re-layouts, body(): jnp.stack(columns, axis=3)  14.7 us
    all_to_all x1, starting transfers between devices, body(): lax.all_to_all(arranged, ('chan', 'band'), split_axis=0, concat_axis=0, t...  10.5 us
    cond x2, local copies, waits for them, and re-layouts, exchange(): return lax.switch(number - 1, branches, rows)  8.87 us
    dot_general x1, matrix products, window_spectrum(): decimated = jnp.dot(piece, table, preferred_element_type=jnp.float32)  7.15 us
    dot_general x1, matrix products, body(): jnp.einsum('qkfi,qkfj->qfij', own, mixed, preferred_element_type=jnp.floa...  6.77 us
    another operation x2, local copies, waits for them, and re-layouts, body(): columns.append(jnp.stack([-imag_rows, real_rows], axis=1))  5.74 us
  transfers between devices with their start and end apart: 3, of which 3 were waited for; matrix products, arithmetic and copies ran while one was open for 0% of the time, Pallas kernels for 0%

profile of v2, /device:TPU:2, one launch (start us, length us, event | category | flops | bytes accessed | tf_op | source)
XLA Modules:
  0.0 169.6 jit_solution(3245230769145969407)
XLA Ops:
  0.0 1.2 sine_negate_fusion
  1.9 0.7 pad.4
  2.6 0.1 reshape.69
  2.7 0.8 convert_bitcast_fusion
  3.5 0.5 convert_element_type.34
  4.0 7.1 %fusion = f32[2560,256]{1,0:T(8,128)S(1)} fusion(bf16[2620,256]{1,0:T(8,128)(2,1)S(1)} %convert_element_type.34, bf16[1,2560,2747]{1,2,0:T(8,128)(2,1)} %param.34, s32[]{:T(128)S(6)} %select_n.13), kind=kOutput, calls=%fused_computation | convolution fusion | flops 3434086400 | bytes 17397764 | tf_op jit(solution)/shard_map/dot_general | solution.py:46
  11.1 0.0 copy-start.5
  11.1 0.0 copy-start.6
  11.1 1.5 fusion.11
  12.6 0.0 copy-done.5
  12.6 0.0 copy-done.6
  12.6 4.4 %convolution_convert_fusion = bf16[256,2560]{1,0:T(8,128)(2,1)S(1)} fusion(f32[2560,256]{1,0:T(8,128)S(1)} %fusion.11, f32[256,128]{1,0:T(8,128)S(1)} %copy-done.5, f32[256,128]{1,0:T(8,128)S(1)} %copy-done.6), kind=kOutput, calls=%fused_computation.14 | convolution fusion | flops 2013986816 | bytes 4194304 | tf_op jit(solution)/shard_map/dot_general | solution.py:51
  17.1 2.6 %convert_element_type.36 = bf16[1,2,8,16,16,160]{5,4,3,2,1,0:T(8,128)(2,1)S(1)} reshape(bf16[256,2560]{1,0:T(8,128)(2,1)S(1)} %convolution_convert_fusion) | data formatting | bytes 2621440 | tf_op jit(solution)/shard_map/convert_element_type | solution.py:54
  19.7 2.0 %copy.26 = bf16[1,2,8,16,16,160]{5,3,1,2,4,0:T(8,128)(2,1)} copy(bf16[1,2,8,16,16,160]{5,4,3,2,1,0:T(8,128)(2,1)S(1)} %convert_element_type.36) | data formatting | bytes 2621440 | tf_op jit(solution)/shard_map/convert_element_type | solution.py:54
  21.7 0.0 copy-start.7
  21.7 10.5 %all-to-all-start = ((bf16[128,2,16,160]{3,2,1,0:T(8,128)(2,1)}), bf16[128,2,16,160]{3,2,1,0:T(8,128)(2,1)S(1)}, u32[]{:S(2)}, u32[]{:S(2)}) async-start(bf16[128,2,16,160]{3,2,1,0:T(8,128)(2,1)} %bitcast.29), calls=%async_computation | async-start | bytes 4194304 | tf_op jit(solution)/shard_map/all_to_all | solution.py:80
  32.2 0.0 copy-done.7
  32.3 0.6 fusion.33
  34.0 27.0 %all-to-all-done = bf16[128,2,16,160]{3,2,1,0:T(8,128)(2,1)S(1)} async-done(((bf16[128,2,16,160]{3,2,1,0:T(8,128)(2,1)}), bf16[128,2,16,160]{3,2,1,0:T(8,128)(2,1)S(1)}, u32[]{:S(2)}, u32[]{:S(2)}) %all-to-all-start) | async-done | bytes 1310752 | tf_op jit(solution)/shard_map/all_to_all | solution.py:80
  61.0 2.8 %copy.28 = bf16[128,2,16,160]{0,3,2,1:T(8,128)(2,1)} copy(bf16[128,2,16,160]{3,2,1,0:T(8,128)(2,1)S(1)} %all-to-all-done) | data formatting | bytes 2621440 | tf_op jit(solution)/shard_map/all_to_all | solution.py:80
  63.9 32.0 %conditional.2 = (bf16[128,2,16,160]{0,3,2,1:T(8,128)(2,1)}) conditional(s32[]{:T(128)} %bitcast.6, bf16[128,2,16,160]{0,3,2,1:T(8,128)(2,1)} %copy.28, bf16[128,2,16,160]{0,3,2,1:T(8,128)(2,1)} %copy.28, bf16[128,2,16,160]{0,3,2,1:T(8,128)(2,1)} %copy.28, bf16[128,2,16,160]{0,3,2,1:T(8,128)(2,1)} %copy.28, ...), branch_computations={%region_0.1_spmd, %region_1.2_spmd, %region_2.3_spmd, %region_3.4_... | conditional | bytes 5242928 | solution.py:90
  63.9 0.7 collective-permute-start.3
  64.6 31.2 %collective-permute-done.3 = bf16[128,2,16,160]{0,3,2,1:T(8,128)(2,1)} collective-permute-done((bf16[128,2,16,160]{0,3,2,1:T(8,128)(2,1)}, bf16[128,2,16,160]{0,3,2,1:T(8,128)(2,1)}, u32[]{:S(2)}, u32[]{:S(2)}) %collective-permute-start.3) | collective-permute-done | bytes 1310752 | tf_op jit(solution)/shard_map/cond/branch_3_fun/ppermute | solution.py:87
  95.9 1.4 slice_negate_fusion.1
  97.3 4.5 %copy.43 = bf16[128,2,16,160]{3,2,1,0:T(8,128)(2,1)} copy(bf16[128,2,16,160]{0,3,2,1:T(8,128)(2,1)} %get-tuple-element.77) | data formatting | bytes 2621440 | tf_op jit(solution)/shard_map/cond | solution.py:90
  101.8 30.5 %conditional.3 = (bf16[128,2,16,160]{0,3,2,1:T(8,128)(2,1)}) conditional(s32[]{:T(128)} %bitcast.9, bf16[128,2,16,160]{0,3,2,1:T(8,128)(2,1)} %copy.28, bf16[128,2,16,160]{0,3,2,1:T(8,128)(2,1)} %copy.28, bf16[128,2,16,160]{0,3,2,1:T(8,128)(2,1)} %copy.28, bf16[128,2,16,160]{0,3,2,1:T(8,128)(2,1)} %copy.28, ...), branch_computations={%region_15.16_spmd, %region_16.17_spmd, %region_17.18_spmd, %regio... | conditional | bytes 5242928 | solution.py:90
  101.8 0.9 collective-permute-start.24
  102.7 29.6 %collective-permute-done.24 = bf16[128,2,16,160]{0,3,2,1:T(8,128)(2,1)} collective-permute-done((bf16[128,2,16,160]{0,3,2,1:T(8,128)(2,1)}, bf16[128,2,16,160]{0,3,2,1:T(8,128)(2,1)}, u32[]{:S(2)}, u32[]{:S(2)}) %collective-permute-start.24) | collective-permute-done | bytes 1310752 | tf_op jit(solution)/shard_map/cond/branch_9_fun/ppermute | solution.py:87
  132.3 2.5 %slice_negate_fusion = (bf16[128,1,16,160]{0,3,2,1:T(8,128)(2,1)}, bf16[128,1,16,160]{0,3,2,1:T(8,128)(2,1)}) fusion(bf16[128,2,16,160]{0,3,2,1:T(8,128)(2,1)} %get-tuple-element.78), kind=kLoop, calls=%fused_computation.24 | loop fusion | flops 327680 | bytes 2621440 | tf_op jit(solution)/shard_map/neg | solution.py:101
  134.8 4.4 %copy.60 = bf16[128,2,16,160]{3,2,1,0:T(8,128)(2,1)} copy(bf16[128,2,16,160]{0,3,2,1:T(8,128)(2,1)} %get-tuple-element.78) | data formatting | bytes 2621440 | tf_op jit(solution)/shard_map/cond | solution.py:90
  139.2 2.8 %copy.27 = bf16[256,16,160]{0,2,1:T(8,128)(2,1)} copy(bf16[256,16,160]{2,1,0:T(8,128)(2,1)S(1)} %bitcast.28) | data formatting | bytes 2621440 | tf_op jit(solution)/shard_map/broadcast_in_dim | solution.py:104
  142.0 0.1 pad_maximum_fusion
  142.1 2.9 %copy.44 = bf16[128,2,16,160]{3,2,1,0:T(8,128)(2,1)} copy(bf16[128,2,16,160]{0,3,2,1:T(8,128)(2,1)S(1)} %pad_maximum_fusion) | data formatting | bytes 2621440 | tf_op jit(solution)/shard_map/stack | solution.py:101
  145.0 0.0 copy-start
  145.0 4.5 %copy.63 = bf16[256,16,1,160]{0,3,1,2:T(8,128)(2,1)} copy(bf16[256,16,1,160]{3,1,0,2:T(8,128)(2,1)} %bitcast.32) | data formatting | bytes 2621440 | tf_op jit(solution)/shard_map/stack | solution.py:102
  149.5 0.0 copy-done
  149.5 0.0 copy-start.2
  149.5 0.0 copy-start.3
  149.6 2.8 %copy.62 = bf16[256,16,1,160]{0,3,1,2:T(8,128)(2,1)} copy(bf16[256,16,1,160]{3,1,0,2:T(8,128)(2,1)S(1)} %bitcast.30) | data formatting | bytes 2621440 | tf_op jit(solution)/shard_map/stack | solution.py:102
  152.4 0.0 copy-done.2
  152.4 0.0 copy-done.3
  152.4 0.1 pad_maximum_fusion.1
  152.5 2.9 %copy.61 = bf16[128,2,16,160]{3,2,1,0:T(8,128)(2,1)} copy(bf16[128,2,16,160]{0,3,2,1:T(8,128)(2,1)S(1)} %pad_maximum_fusion.1) | data formatting | bytes 2621440 | tf_op jit(solution)/shard_map/stack | solution.py:101
  155.4 0.0 copy-start.1
  155.4 4.6 %copy.65 = bf16[256,16,1,160]{0,3,1,2:T(8,128)(2,1)} copy(bf16[256,16,1,160]{3,1,0,2:T(8,128)(2,1)} %bitcast.33) | data formatting | bytes 2621440 | tf_op jit(solution)/shard_map/stack | solution.py:102
  160.0 0.0 copy-done.1
  160.0 0.0 copy-start.4
  160.0 2.8 %copy.64 = bf16[256,16,1,160]{0,3,1,2:T(8,128)(2,1)} copy(bf16[256,16,1,160]{3,1,0,2:T(8,128)(2,1)S(1)} %bitcast.31) | data formatting | bytes 2621440 | tf_op jit(solution)/shard_map/stack | solution.py:102
  162.8 0.0 copy-done.4
  162.8 6.8 %broadcast_multiply_fusion = f32[4,16,160,160]{3,2,1,0:T(8,128)} fusion(bf16[256,16,1,160]{0,3,1,2:T(8,128)(2,1)} %copy.65, bf16[256,16,1,160]{0,3,1,2:T(8,128)(2,1)} %copy.64, bf16[256,16,1,160]{0,3,1,2:T(8,128)(2,1)} %copy.63, bf16[256,16,1,160]{0,3,1,2:T(8,128)(2,1)} %copy.62, bf16[256,16,160]{0,2,1:T(8,128)(2,1)S(1)} %copy-done.4), kind=kOutput, calls=%fused_computation.11 | convolution fusion | flops 848363520 | bytes 13107200 | tf_op jit(solution)/shard_map/qkfi,qkfj->qfij/dot_general | solution.py:106
  (2 shorter events, 0.0 us)
Async XLA Ops:
  11.1 1.5 copy-start.5
  11.1 1.5 copy-start.6
  21.7 10.5 %copy-start.7 = (s32[2,16]{1,0:T(2,128)S(1)}, s32[2,16]{1,0:T(2,128)}, u32[]{:S(2)}) copy-start(s32[2,16]{1,0:T(2,128)} %param.37) | copy-start | bytes 388
  21.7 39.3 %all-to-all-start = ((bf16[128,2,16,160]{3,2,1,0:T(8,128)(2,1)}), bf16[128,2,16,160]{3,2,1,0:T(8,128)(2,1)S(1)}, u32[]{:S(2)}, u32[]{:S(2)}) async-start(bf16[128,2,16,160]{3,2,1,0:T(8,128)(2,1)} %bitcast.29), calls=%async_computation | async-start | bytes 4194304 | tf_op jit(solution)/shard_map/all_to_all | solution.py:80
  63.9 32.0 %collective-permute-start.3 = (bf16[128,2,16,160]{0,3,2,1:T(8,128)(2,1)}, bf16[128,2,16,160]{0,3,2,1:T(8,128)(2,1)}, u32[]{:S(2)}, u32[]{:S(2)}) collective-permute-start(bf16[128,2,16,160]{0,3,2,1:T(8,128)(2,1)} %param.3), channel_id=1, source_target_pairs={{0,32},{8,40},{16,48},{24,56},{32,0},{40,8},{48,16},{56,24},{64,96... | collective-permute-start | bytes 3932168 | tf_op jit(solution)/shard_map/cond/branch_3_fun/ppermute | solution.py:87
  101.8 30.5 %collective-permute-start.24 = (bf16[128,2,16,160]{0,3,2,1:T(8,128)(2,1)}, bf16[128,2,16,160]{0,3,2,1:T(8,128)(2,1)}, u32[]{:S(2)}, u32[]{:S(2)}) collective-permute-start(bf16[128,2,16,160]{0,3,2,1:T(8,128)(2,1)} %param.24), channel_id=1, source_target_pairs={{0,80},{8,88},{16,64},{24,72},{32,112},{40,120},{48,96},{56,104},{... | collective-permute-start | bytes 3932168 | tf_op jit(solution)/shard_map/cond/branch_9_fun/ppermute | solution.py:87
  145.0 4.5 %copy-start = (bf16[128,2,16,160]{3,2,1,0:T(8,128)(2,1)S(1)}, bf16[128,2,16,160]{3,2,1,0:T(8,128)(2,1)}, u32[]{:S(2)}) copy-start(bf16[128,2,16,160]{3,2,1,0:T(8,128)(2,1)} %copy.43) | copy-start | bytes 3932164
  149.5 2.8 %copy-start.2 = (bf16[128,1,16,160]{0,3,2,1:T(8,128)(2,1)S(1)}, bf16[128,1,16,160]{0,3,2,1:T(8,128)(2,1)}, u32[]{:S(2)}) copy-start(bf16[128,1,16,160]{0,3,2,1:T(8,128)(2,1)} %get-tuple-element.69) | copy-start | bytes 1966084
  149.5 2.8 %copy-start.3 = (bf16[128,1,16,160]{0,3,2,1:T(8,128)(2,1)S(1)}, bf16[128,1,16,160]{0,3,2,1:T(8,128)(2,1)}, u32[]{:S(2)}) copy-start(bf16[128,1,16,160]{0,3,2,1:T(8,128)(2,1)} %get-tuple-element.70) | copy-start | bytes 1966084
  155.4 4.6 %copy-start.1 = (bf16[128,2,16,160]{3,2,1,0:T(8,128)(2,1)S(1)}, bf16[128,2,16,160]{3,2,1,0:T(8,128)(2,1)}, u32[]{:S(2)}) copy-start(bf16[128,2,16,160]{3,2,1,0:T(8,128)(2,1)} %copy.60) | copy-start | bytes 3932164
  160.0 2.8 %copy-start.4 = (bf16[256,16,160]{0,2,1:T(8,128)(2,1)S(1)}, bf16[256,16,160]{0,2,1:T(8,128)(2,1)}, u32[]{:S(2)}) copy-start(bf16[256,16,160]{0,2,1:T(8,128)(2,1)} %copy.27) | copy-start | bytes 3932164

commit v3 on v2

--- a/solution.py
+++ b/solution.py
@@ -59,51 +59,36 @@
     table = filter_table(taps, phases)
     level_matrix = mean_matrix(W, HALF)
     transform = dft_table(W, NF)
-    spectra = jnp.stack([window_spectrum(raw[0], offsets[0], table, level_matrix, transform)])
+    spectrum = window_spectrum(raw[0], offsets[0], table, level_matrix, transform)
     chan_count = lax.axis_size("chan")
     band_count = lax.axis_size("band")
-    window_count, part_count, bin_count, channel_count = spectra.shape
-    arranged = spectra.reshape(
-        window_count,
-        part_count,
-        band_count,
-        bin_count // band_count,
-        chan_count,
-        channel_count // chan_count,
+    part_count, bin_count, channel_count = spectrum.shape
+    bins = bin_count // band_count
+    width = channel_count // chan_count
+    arranged = spectrum.reshape(part_count, band_count, bins, chan_count, width)
+    arranged = arranged.transpose(0, 2, 4, 3, 1).reshape(
+        part_count, bins, width, chan_count * band_count
     )
-    arranged = arranged.transpose(4, 2, 0, 1, 3, 5).reshape(
-        chan_count * band_count * window_count,
-        part_count,
-        bin_count // band_count,
-        channel_count // chan_count,
-    )
-    local = lax.all_to_all(arranged, ("chan", "band"), split_axis=0, concat_axis=0, tiled=True)
-    width = local.shape[3]
-    chan_count_static = chan_count
+    local = lax.all_to_all(arranged, ("chan", "band"), split_axis=3, concat_axis=3, tiled=True)
 
     def exchange(rows, number):
         def branch(shift):
-            pairs = [(a, a ^ shift) for a in range(chan_count_static)]
+            pairs = [(a, a ^ shift) for a in range(chan_count)]
             return lambda x: lax.ppermute(x, "chan", pairs)
 
-        branches = [branch(shift) for shift in range(1, chan_count_static)]
+        branches = [branch(shift) for shift in range(1, chan_count)]
         return lax.switch(number - 1, branches, rows)
 
     first_other = exchange(local, partner[0, 0])
     second_other = exchange(local, partner[1, 0])
-    factor = 1.0 / (W * math.sqrt(local.shape[0]))
-    windows, parts, bins, width = local.shape
+    factor = 1.0 / (W * math.sqrt(local.shape[3]))
     columns = []
     for other_rows in (first_other, second_other):
-        real_rows = other_rows[:, 0]
-        imag_rows = other_rows[:, 1]
         columns.append(other_rows)
-        columns.append(jnp.stack([-imag_rows, real_rows], axis=1))
-    mixed = jnp.stack(columns, axis=3).reshape(windows * parts, bins, len(columns), width)
-    own = local.reshape(windows * parts, bins, width)
-    own = jnp.broadcast_to(own[None], (len(columns),) + own.shape)
-    mixed = jnp.moveaxis(mixed, 2, 0)
-    product = jnp.einsum("qkfi,qkfj->qfij", own, mixed, preferred_element_type=jnp.float32)
+        columns.append(jnp.stack([-other_rows[1], other_rows[0]]))
+    mixed = jnp.stack(columns)
+    own = jnp.broadcast_to(local[None], mixed.shape)
+    product = jnp.einsum("qpfiw,qpfjw->qfij", own, mixed, preferred_element_type=jnp.float32)
     return (product * factor).reshape(2, 2, bins, width, width)
 
 

time: 172 us -> 144 us (0.84)
  local copies, waits for them, and re-layouts: 41.4 us -> 16.5 us
    another operation x6 -> x0, local copies, waits for them, and re-layouts: 20.5 us -> none  [the longest x4 14.7 us: body(): jnp.stack(columns, axis=3)]
    cond x2, local copies, waits for them, and re-layouts: 8.87 us -> 2.88 us  [exchange(): return lax.switch(number - 1, branches, rows)]
    neg x2, other arithmetic: 3.96 us -> 0.26 us  [body(): columns.append(jnp.stack([-other_rows[1], other_rows[0]]))]
    broadcast_in_dim x1 -> x0, local copies, waits for them, and re-layouts: 2.78 us -> none  [body(): own = jnp.broadcast_to(own[None], (len(columns),) + own.shape)]
    reshape x0 -> x1, local copies, waits for them, and re-layouts: none -> 2.51 us  [body(): arranged.transpose(0, 2, 4, 3, 1)]
    another operation x2, other arithmetic: 0.24 us -> 2.4 us  [body(): mixed = jnp.stack(columns)]
    all_to_all x1 -> x2, local copies, waits for them, and re-layouts: 2.84 us -> 4.85 us  [body(): lax.all_to_all(arranged, ('chan', 'band'), split_axis=3, concat_axis=3, t...]
where the time goes in v3:
time: 144 us; the launch traced here: 142 us
  waiting for transfers between devices  87 us (60%)
  matrix products  20.6 us (14%)
  local copies, waits for them, and re-layouts  16.5 us (11%)
  starting transfers between devices  11.5 us (8%)
  other arithmetic  3.92 us (3%)
  between operations  2.03 us (1%)
    ppermute x2, waiting for transfers between devices, branch(): return lambda x: lax.ppermute(x, 'chan', pairs)  60 us
    all_to_all x1, waiting for transfers between devices, body(): lax.all_to_all(arranged, ('chan', 'band'), split_axis=3, concat_axis=3, t...  27 us
    all_to_all x1, starting transfers between devices, body(): lax.all_to_all(arranged, ('chan', 'band'), split_axis=3, concat_axis=3, t...  10.5 us
    dot_general x1, matrix products, window_spectrum(): decimated = jnp.dot(piece, table, preferred_element_type=jnp.float32)  7.15 us
    dot_general x1, matrix products, body(): jnp.einsum('qpfiw,qpfjw->qfij', own, mixed, preferred_element_type=jnp.fl...  6.74 us
    all_to_all x2, local copies, waits for them, and re-layouts, body(): lax.all_to_all(arranged, ('chan', 'band'), split_axis=3, concat_axis=3, t...  4.85 us
    convert_element_type x2, local copies, waits for them, and re-layouts, window_spectrum(): return spectrum.reshape(2, NF, segment.shape[0]).astype(jnp.bfloat16)  4.52 us
    dot_general x1, matrix products, window_spectrum(): lax.dot_general(transform, normed, (((0,), (1,)), ((), ())), precision=la...  4.41 us
  transfers between devices with their start and end apart: 3, of which 3 were waited for; matrix products, arithmetic and copies ran while one was open for 0% of the time, Pallas kernels for 0%

profile of v3, /device:TPU:2, one launch (start us, length us, event | category | flops | bytes accessed | tf_op | source)
XLA Modules:
  0.0 141.6 jit_solution(15938660864524311555)
XLA Ops:
  0.0 1.2 sine_negate_fusion
  1.9 0.7 pad.4
  2.6 0.1 reshape.52
  2.7 0.8 convert_bitcast_fusion
  3.5 0.5 convert_element_type.28
  4.0 7.1 %fusion = f32[2560,256]{1,0:T(8,128)S(1)} fusion(bf16[2620,256]{1,0:T(8,128)(2,1)S(1)} %convert_element_type.28, bf16[1,2560,2747]{1,2,0:T(8,128)(2,1)} %param.34, s32[]{:T(128)S(6)} %select_n.13), kind=kOutput, calls=%fused_computation | convolution fusion | flops 3434086400 | bytes 17397764 | tf_op jit(solution)/shard_map/dot_general | solution.py:46
  11.1 0.0 copy-start.1
  11.1 0.0 copy-start.2
  11.1 1.5 %fusion.12 = f32[2560,256]{1,0:T(8,128)S(1)} fusion(f32[2560,256]{1,0:T(8,128)S(1)} %fusion, s32[256]{0:T(256)S(1)} %get-tuple-element.78, s32[256]{0:T(256)S(1)} %get-tuple-element.77), kind=kOutput, calls=%fused_computation.15 | convolution fusion | flops 2016083968 | bytes 5244928 | tf_op jit(solution)/shard_map/dot_general | solution.py:47
  12.6 0.0 copy-done.1
  12.6 0.0 copy-done.2
  12.6 4.4 %convolution_convert_fusion = bf16[256,2560]{1,0:T(8,128)(2,1)S(1)} fusion(f32[2560,256]{1,0:T(8,128)S(1)} %fusion.12, f32[256,128]{1,0:T(8,128)S(1)} %copy-done.1, f32[256,128]{1,0:T(8,128)S(1)} %copy-done.2), kind=kOutput, calls=%fused_computation.14 | convolution fusion | flops 2013986816 | bytes 4194304 | tf_op jit(solution)/shard_map/dot_general | solution.py:51
  17.1 2.8 %convert_element_type.30 = bf16[2,8,16,16,160]{4,3,2,1,0:T(8,128)(2,1)S(1)} reshape(bf16[256,2560]{1,0:T(8,128)(2,1)S(1)} %convolution_convert_fusion) | data formatting | bytes 2621440 | tf_op jit(solution)/shard_map/convert_element_type | solution.py:54
  19.9 1.7 %copy.96 = bf16[2,8,16,16,160]{4,1,3,2,0:T(8,128)(2,1)S(1)} copy(bf16[2,8,16,16,160]{4,3,2,1,0:T(8,128)(2,1)S(1)} %convert_element_type.30) | data formatting | bytes 2621440 | tf_op jit(solution)/shard_map/convert_element_type | solution.py:54
  21.6 2.5 %copy.52 = bf16[2,16,160,128]{2,1,0,3:T(8,128)(2,1)} copy(bf16[2,16,160,128]{2,3,1,0:T(8,128)(2,1)S(1)} %bitcast.33) | data formatting | bytes 2621440 | tf_op jit(solution)/shard_map/reshape | solution.py:69
  24.1 0.0 copy-start.3
  24.1 10.5 %all-to-all-start = ((bf16[2,16,160,128]{2,1,0,3:T(8,128)(2,1)}), bf16[2,16,160,128]{2,1,0,3:T(8,128)(2,1)S(1)}, u32[]{:S(2)}, u32[]{:S(2)}) async-start(bf16[2,16,160,128]{2,1,0,3:T(8,128)(2,1)} %copy.52), calls=%async_computation | async-start | bytes 4194304 | tf_op jit(solution)/shard_map/all_to_all | solution.py:72
  34.6 0.0 copy-done.3
  34.6 0.6 fusion.36
  36.4 27.0 %all-to-all-done = bf16[2,16,160,128]{2,1,0,3:T(8,128)(2,1)S(1)} async-done(((bf16[2,16,160,128]{2,1,0,3:T(8,128)(2,1)}), bf16[2,16,160,128]{2,1,0,3:T(8,128)(2,1)S(1)}, u32[]{:S(2)}, u32[]{:S(2)}) %all-to-all-start) | async-done | bytes 1310752 | tf_op jit(solution)/shard_map/all_to_all | solution.py:72
  63.4 2.0 %copy.54 = bf16[2,16,160,128]{3,2,1,0:T(8,128)(2,1)S(1)} copy(bf16[2,16,160,128]{2,1,0,3:T(8,128)(2,1)S(1)} %all-to-all-done) | data formatting | bytes 2621440 | tf_op jit(solution)/shard_map/all_to_all | solution.py:72
  65.4 31.6 %conditional.3 = (bf16[2,16,160,128]{3,2,1,0:T(8,128)(2,1)}) conditional(s32[]{:T(128)} %bitcast.8, bf16[2,16,160,128]{3,2,1,0:T(8,128)(2,1)S(1)} %copy.54, bf16[2,16,160,128]{3,2,1,0:T(8,128)(2,1)S(1)} %copy.54, bf16[2,16,160,128]{3,2,1,0:T(8,128)(2,1)S(1)} %copy.54, ...), branch_computations={%region_15.16_spmd, %region_16.17_spmd, %region_17.18_spmd, %regio... | conditional | bytes 5242928 | solution.py:80
  65.4 1.0 collective-permute-start.20
  66.5 30.6 %collective-permute-done.20 = bf16[2,16,160,128]{3,2,1,0:T(8,128)(2,1)} collective-permute-done((bf16[2,16,160,128]{3,2,1,0:T(8,128)(2,1)S(1)}, bf16[2,16,160,128]{3,2,1,0:T(8,128)(2,1)}, u32[]{:S(2)}, u32[]{:S(2)}) %collective-permute-start.20) | collective-permute-done | bytes 1310752 | tf_op jit(solution)/shard_map/cond/branch_5_fun/ppermute | solution.py:77
  97.0 29.4 %conditional.2 = (bf16[2,16,160,128]{3,2,1,0:T(8,128)(2,1)}) conditional(s32[]{:T(128)} %bitcast.5, bf16[2,16,160,128]{3,2,1,0:T(8,128)(2,1)S(1)} %copy.54, bf16[2,16,160,128]{3,2,1,0:T(8,128)(2,1)S(1)} %copy.54, bf16[2,16,160,128]{3,2,1,0:T(8,128)(2,1)S(1)} %copy.54, ...), branch_computations={%region_0.1_spmd, %region_1.2_spmd, %region_2.3_spmd, %region_3.4_... | conditional | bytes 5242928 | solution.py:80
  97.0 0.0 collective-permute-start.1
  97.0 29.4 %collective-permute-done.1 = bf16[2,16,160,128]{3,2,1,0:T(8,128)(2,1)} collective-permute-done((bf16[2,16,160,128]{3,2,1,0:T(8,128)(2,1)S(1)}, bf16[2,16,160,128]{3,2,1,0:T(8,128)(2,1)}, u32[]{:S(2)}, u32[]{:S(2)}) %collective-permute-start.1) | collective-permute-done | bytes 1310752 | tf_op jit(solution)/shard_map/cond/branch_1_fun/ppermute | solution.py:77
  126.4 1.4 %copy.98 = bf16[2,16,160,128]{3,2,0,1:T(8,128)(2,1)S(1)} copy(bf16[2,16,160,128]{3,2,1,0:T(8,128)(2,1)} %get-tuple-element.81) | data formatting | bytes 2621440 | tf_op jit(solution)/shard_map/cond | solution.py:80
  127.9 1.4 %copy.97 = bf16[2,16,160,128]{3,2,0,1:T(8,128)(2,1)S(1)} copy(bf16[2,16,160,128]{3,2,1,0:T(8,128)(2,1)} %get-tuple-element.82) | data formatting | bytes 2621440 | tf_op jit(solution)/shard_map/cond | solution.py:80
  129.3 0.0 copy-start
  129.3 0.1 slice_negate_fusion
  129.5 0.1 slice_negate_fusion.1
  129.6 1.2 maximum_bitcast_fusion.1
  130.8 0.0 copy-done
  130.8 1.2 maximum_bitcast_fusion
  132.0 2.9 %copy.53 = bf16[2,16,160,128]{3,2,0,1:T(8,128)(2,1)} copy(bf16[2,16,160,128]{2,1,0,3:T(8,128)(2,1)S(1)} %all-to-all-done) | data formatting | bytes 2621440 | tf_op jit(solution)/shard_map/all_to_all | solution.py:72
  134.9 6.7 %bitcast_multiply_fusion = f32[4,16,160,160]{3,2,1,0:T(8,128)} fusion(bf16[1,2,16,160,128]{4,3,1,2,0:T(8,128)(2,1)} %maximum_bitcast_fusion.1, bf16[1,2,16,160,128]{4,3,1,2,0:T(8,128)(2,1)} %bitcast.35, bf16[1,2,16,160,128]{4,3,1,2,0:T(8,128)(2,1)} %maximum_bitcast_fusion, bf16[1,2,16,160,128]{4,3,1,2,0:T(8,128)(2,1)S(1)} %bitcast.34, ...), kind=kOutput, calls=%fused_computation.3 | convolution fusion | flops 848363520 | bytes 13107200 | tf_op jit(solution)/shard_map/qpfiw,qpfjw->qfij/dot_general | solution.py:91
  (2 shorter events, 0.0 us)
Async XLA Ops:
  11.1 1.5 %copy-start.1 = (f32[256,128]{1,0:T(8,128)S(1)}, f32[256,128]{1,0:T(8,128)}, u32[]{:S(2)}) copy-start(f32[256,128]{1,0:T(8,128)} %get-tuple-element.79) | copy-start | bytes 393220
  11.1 1.5 %copy-start.2 = (f32[256,128]{1,0:T(8,128)S(1)}, f32[256,128]{1,0:T(8,128)}, u32[]{:S(2)}) copy-start(f32[256,128]{1,0:T(8,128)} %get-tuple-element.80) | copy-start | bytes 393220
  24.1 10.5 %copy-start.3 = (s32[2,16]{1,0:T(2,128)S(1)}, s32[2,16]{1,0:T(2,128)}, u32[]{:S(2)}) copy-start(s32[2,16]{1,0:T(2,128)} %param.37) | copy-start | bytes 388
  24.1 39.3 %all-to-all-start = ((bf16[2,16,160,128]{2,1,0,3:T(8,128)(2,1)}), bf16[2,16,160,128]{2,1,0,3:T(8,128)(2,1)S(1)}, u32[]{:S(2)}, u32[]{:S(2)}) async-start(bf16[2,16,160,128]{2,1,0,3:T(8,128)(2,1)} %copy.52), calls=%async_computation | async-start | bytes 4194304 | tf_op jit(solution)/shard_map/all_to_all | solution.py:72
  65.4 31.6 %collective-permute-start.20 = (bf16[2,16,160,128]{3,2,1,0:T(8,128)(2,1)S(1)}, bf16[2,16,160,128]{3,2,1,0:T(8,128)(2,1)}, u32[]{:S(2)}, u32[]{:S(2)}) collective-permute-start(bf16[2,16,160,128]{3,2,1,0:T(8,128)(2,1)S(1)} %param.20), channel_id=1, source_target_pairs={{0,48},{8,56},{16,32},{24,40},{32,16},{40,24},{48,0},{56,8},{64,11... | collective-permute-start | bytes 3932168 | tf_op jit(solution)/shard_map/cond/branch_5_fun/ppermute | solution.py:77
  97.0 29.4 %collective-permute-start.1 = (bf16[2,16,160,128]{3,2,1,0:T(8,128)(2,1)S(1)}, bf16[2,16,160,128]{3,2,1,0:T(8,128)(2,1)}, u32[]{:S(2)}, u32[]{:S(2)}) collective-permute-start(bf16[2,16,160,128]{3,2,1,0:T(8,128)(2,1)S(1)} %param.1), channel_id=1, source_target_pairs={{0,16},{8,24},{16,0},{24,8},{32,48},{40,56},{48,32},{56,40},{64,80... | collective-permute-start | bytes 3932168 | tf_op jit(solution)/shard_map/cond/branch_1_fun/ppermute | solution.py:77
  129.3 1.5 %copy-start = (bf16[2,16,160,128]{3,2,0,1:T(8,128)(2,1)}, bf16[2,16,160,128]{3,2,0,1:T(8,128)(2,1)S(1)}, u32[]{:S(2)}) copy-start(bf16[2,16,160,128]{3,2,0,1:T(8,128)(2,1)S(1)} %copy.97) | copy-start | bytes 3932164

commit v4 on v3

--- a/solution.py
+++ b/solution.py
@@ -40,18 +40,34 @@
     return table.reshape((W + phases - 1) * DEC, W).astype(jnp.bfloat16)
 
 
-def window_spectrum(segment, offset, table, level_matrix, transform):
+def window_spectrum(segment, offset, table, level_matrix, transform, blocks, bands):
     span = table.shape[0]
-    piece = lax.dynamic_slice_in_dim(segment, offset, span, 1)
-    decimated = jnp.dot(piece, table, preferred_element_type=jnp.float32)
+    half = W // 2
+    rows = span - half * DEC
+    decimated = jnp.concatenate(
+        [
+            jnp.dot(
+                lax.dynamic_slice_in_dim(segment, offset + start * DEC, rows, 1),
+                table[start * DEC : start * DEC + rows, start : start + half],
+                preferred_element_type=jnp.float32,
+            )
+            for start in (0, half)
+        ],
+        axis=1,
+    )
     level = jnp.dot(jnp.abs(decimated), level_matrix, precision=lax.Precision.HIGHEST) / (
         2 * HALF + 1
     )
     normed = decimated / (level + 1e-05)
-    spectrum = lax.dot_general(
-        transform, normed, (((0,), (1,)), ((), ())), precision=lax.Precision.HIGHEST
+    channels = segment.shape[0]
+    ordered = transform.reshape(W, 2, bands, NF // bands).transpose(0, 2, 1, 3).reshape(W, 2 * NF)
+    spectrum = jnp.einsum(
+        "ain,nk->aki",
+        normed.reshape(blocks, channels // blocks, W),
+        ordered,
+        precision=lax.Precision.HIGHEST,
     )
-    return spectrum.reshape(2, NF, segment.shape[0]).astype(jnp.bfloat16)
+    return spectrum.reshape(blocks, bands, 2, NF // bands, channels // blocks).astype(jnp.bfloat16)
 
 
 def body(raw, offsets, taps, partner):
@@ -59,14 +75,13 @@
     table = filter_table(taps, phases)
     level_matrix = mean_matrix(W, HALF)
     transform = dft_table(W, NF)
-    spectrum = window_spectrum(raw[0], offsets[0], table, level_matrix, transform)
     chan_count = lax.axis_size("chan")
     band_count = lax.axis_size("band")
-    part_count, bin_count, channel_count = spectrum.shape
-    bins = bin_count // band_count
-    width = channel_count // chan_count
-    arranged = spectrum.reshape(part_count, band_count, bins, chan_count, width)
-    arranged = arranged.transpose(0, 2, 4, 3, 1).reshape(
+    spectrum = window_spectrum(
+        raw[0], offsets[0], table, level_matrix, transform, chan_count, band_count
+    )
+    _, _, part_count, bins, width = spectrum.shape
+    arranged = spectrum.transpose(2, 3, 4, 0, 1).reshape(
         part_count, bins, width, chan_count * band_count
     )
     local = lax.all_to_all(arranged, ("chan", "band"), split_axis=3, concat_axis=3, tiled=True)

time: 144 us -> 148 us (1.028)
  matrix products: 20.6 us -> 24.6 us
    reshape x1 -> x0, local copies, waits for them, and re-layouts: 2.51 us -> none  [body(): arranged.transpose(0, 2, 4, 3, 1)]
    div x0 -> x1, local copies, waits for them, and re-layouts: none -> 2.19 us  [window_spectrum(): normed = decimated / (level + 1e-05)]
    dot_general x2 -> x3, matrix products: 11.6 us -> 13.6 us  [the longest x2 10.3 us: window_spectrum(): jnp.dot(lax.dynamic_slice_in_dim(segment, offset + start * DEC, rows, 1),...]
    dot_general x1, matrix products: 1.47 us -> 3.41 us  [window_spectrum(): jnp.dot(jnp.abs(decimated), level_matrix, precision=lax.Precision.HIGHEST)]
    convert_element_type x2 -> x1, local copies, waits for them, and re-layouts: 4.52 us -> 3.59 us  [window_spectrum(): spectrum.reshape(blocks, bands, 2, NF // bands, channels // blocks)]
where the time goes in v4:
time: 148 us; the launch traced here: 146 us
  waiting for transfers between devices  87.4 us (59%)
  matrix products  24.6 us (17%)
  local copies, waits for them, and re-layouts  16.2 us (11%)
  starting transfers between devices  11.4 us (8%)
  other arithmetic  4 us (3%)
  between operations  2.02 us (1%)
    ppermute x2, waiting for transfers between devices, branch(): return lambda x: lax.ppermute(x, 'chan', pairs)  60.4 us
    all_to_all x1, waiting for transfers between devices, body(): lax.all_to_all(arranged, ('chan', 'band'), split_axis=3, concat_axis=3, t...  27 us
    all_to_all x1, starting transfers between devices, body(): lax.all_to_all(arranged, ('chan', 'band'), split_axis=3, concat_axis=3, t...  10.5 us
    dot_general x2, matrix products, window_spectrum(): jnp.dot(lax.dynamic_slice_in_dim(segment, offset + start * DEC, rows, 1),...  10.3 us
    dot_general x1, matrix products, body(): jnp.einsum('qpfiw,qpfjw->qfij', own, mixed, preferred_element_type=jnp.fl...  6.74 us
    all_to_all x2, local copies, waits for them, and re-layouts, body(): lax.all_to_all(arranged, ('chan', 'band'), split_axis=3, concat_axis=3, t...  4.85 us
    convert_element_type x1, local copies, waits for them, and re-layouts, window_spectrum(): spectrum.reshape(blocks, bands, 2, NF // bands, channels // blocks)  3.59 us
    dot_general x1, matrix products, window_spectrum(): jnp.dot(jnp.abs(decimated), level_matrix, precision=lax.Precision.HIGHEST)  3.41 us
  transfers between devices with their start and end apart: 3, of which 3 were waited for; matrix products, arithmetic and copies ran while one was open for 0% of the time, Pallas kernels for 0%

profile of v4, /device:TPU:2, one launch (start us, length us, event | category | flops | bytes accessed | tf_op | source)
XLA Modules:
  0.0 145.7 jit_solution(13741562566172389426)
XLA Ops:
  0.7 0.7 pad.4
  1.4 0.1 reshape.138
  1.4 1.3 fusion.35
  2.7 0.8 convert_bitcast_fusion
  3.6 0.5 convert_element_type.41
  4.0 5.1 %fusion = f32[2560,128]{0,1:T(8,128)S(1)} fusion(bf16[1,2560,2747]{1,2,0:T(8,128)(2,1)} %param.34, s32[]{:T(128)S(6)} %select_n.28, bf16[2620,256]{1,0:T(8,128)(2,1)S(1)} %convert_element_type.41), kind=kOutput, calls=%fused_computation.1 | convolution fusion | flops 878182400 | bytes 8536068 | tf_op jit(solution)/shard_map/dot_general | solution.py:49
  9.2 5.1 %fusion.2 = f32[2560,128]{0,1:T(8,128)S(1)} fusion(bf16[1,2560,2747]{1,2,0:T(8,128)(2,1)} %param.34, s32[]{:T(128)S(6)} %select_n.27, bf16[2620,256]{1,0:T(8,128)(2,1)S(1)} %convert_element_type.41), kind=kOutput, calls=%fused_computation.3 | convolution fusion | flops 878182400 | bytes 8536068 | tf_op jit(solution)/shard_map/dot_general | solution.py:49
  14.3 3.4 %fusion.15 = f32[2560,256]{0,1:T(8,128)} fusion(f32[2560,128]{0,1:T(8,128)S(1)} %fusion, f32[2560,128]{0,1:T(8,128)S(1)} %fusion.2, s32[256]{0:T(256)S(1)} %get-tuple-element.80, s32[256]{0:T(256)S(1)} %get-tuple-element.79), kind=kOutput, calls=%fused_computation.17 | convolution fusion | flops 2017394688 | bytes 5244928 | tf_op jit(solution)/shard_map/dot_general | solution.py:58
  17.8 0.0 copy-start.1
  17.8 0.0 copy-start.2
  17.8 2.2 %copy.58 = f32[2560,256]{1,0:T(8,128)S(1)} copy(f32[2560,256]{0,1:T(8,128)} %fusion.15) | data formatting | bytes 5242880 | tf_op jit(solution)/shard_map/div | solution.py:61
  20.0 0.0 copy-done.1
  20.0 0.0 copy-done.2
  20.0 3.3 %fusion.21 = bf16[16,256,160]{1,2,0:T(8,128)(2,1)} fusion(f32[256,256,1]{0,1,2:T(8,128)S(1)} %bitcast.50, f32[16,160,256]{2,1,0:T(8,128)S(1)} %bitcast.46), kind=kOutput, calls=%fused_computation.25 | convolution fusion | flops 2013921280 | bytes 4194304 | tf_op jit(solution)/shard_map/ain,nk->aki/dot_general | solution.py:64
  23.4 3.6 %copy.60 = bf16[16,256,160]{2,1,0:T(8,128)(2,1)} copy(bf16[16,256,160]{1,2,0:T(8,128)(2,1)} %fusion.21) | data formatting | bytes 2621440 | tf_op jit(solution)/shard_map/convert_element_type | solution.py:70
  26.9 0.0 copy-start.3
  26.9 10.5 %all-to-all-start = ((bf16[2,16,160,128]{2,1,0,3:T(8,128)(2,1)}), bf16[2,16,160,128]{2,1,0,3:T(8,128)(2,1)S(1)}, u32[]{:S(2)}, u32[]{:S(2)}) async-start(bf16[2,16,160,128]{2,1,0,3:T(8,128)(2,1)} %bitcast.47), calls=%async_computation | async-start | bytes 4194304 | tf_op jit(solution)/shard_map/all_to_all | solution.py:87
  37.5 0.0 copy-done.3
  37.5 0.6 fusion.40
  39.3 27.0 %all-to-all-done = bf16[2,16,160,128]{2,1,0,3:T(8,128)(2,1)S(1)} async-done(((bf16[2,16,160,128]{2,1,0,3:T(8,128)(2,1)}), bf16[2,16,160,128]{2,1,0,3:T(8,128)(2,1)S(1)}, u32[]{:S(2)}, u32[]{:S(2)}) %all-to-all-start) | async-done | bytes 1310752 | tf_op jit(solution)/shard_map/all_to_all | solution.py:87
  66.3 2.0 %copy.64 = bf16[2,16,160,128]{3,2,1,0:T(8,128)(2,1)S(1)} copy(bf16[2,16,160,128]{2,1,0,3:T(8,128)(2,1)S(1)} %all-to-all-done) | data formatting | bytes 2621440 | tf_op jit(solution)/shard_map/all_to_all | solution.py:87
  68.3 30.4 %conditional.3 = (bf16[2,16,160,128]{3,2,1,0:T(8,128)(2,1)}) conditional(s32[]{:T(128)} %bitcast.15, bf16[2,16,160,128]{3,2,1,0:T(8,128)(2,1)S(1)} %copy.64, bf16[2,16,160,128]{3,2,1,0:T(8,128)(2,1)S(1)} %copy.64, bf16[2,16,160,128]{3,2,1,0:T(8,128)(2,1)S(1)} %copy.64, ...), branch_computations={%region_15.16_spmd, %region_16.17_spmd, %region_17.18_spmd, %regio... | conditional | bytes 5242928 | solution.py:95
  68.3 0.9 collective-permute-start.16
  69.2 29.5 %collective-permute-done.16 = bf16[2,16,160,128]{3,2,1,0:T(8,128)(2,1)} collective-permute-done((bf16[2,16,160,128]{3,2,1,0:T(8,128)(2,1)S(1)}, bf16[2,16,160,128]{3,2,1,0:T(8,128)(2,1)}, u32[]{:S(2)}, u32[]{:S(2)}) %collective-permute-start.16) | collective-permute-done | bytes 1310752 | tf_op jit(solution)/shard_map/cond/branch_1_fun/ppermute | solution.py:92
  98.6 30.9 %conditional.2 = (bf16[2,16,160,128]{3,2,1,0:T(8,128)(2,1)}) conditional(s32[]{:T(128)} %bitcast.12, bf16[2,16,160,128]{3,2,1,0:T(8,128)(2,1)S(1)} %copy.64, bf16[2,16,160,128]{3,2,1,0:T(8,128)(2,1)S(1)} %copy.64, bf16[2,16,160,128]{3,2,1,0:T(8,128)(2,1)S(1)} %copy.64, ...), branch_computations={%region_0.1_spmd, %region_1.2_spmd, %region_2.3_spmd, %region_3.4_... | conditional | bytes 5242928 | solution.py:95
  98.6 0.0 collective-permute-start.10
  98.7 30.9 %collective-permute-done.10 = bf16[2,16,160,128]{3,2,1,0:T(8,128)(2,1)} collective-permute-done((bf16[2,16,160,128]{3,2,1,0:T(8,128)(2,1)S(1)}, bf16[2,16,160,128]{3,2,1,0:T(8,128)(2,1)}, u32[]{:S(2)}, u32[]{:S(2)}) %collective-permute-start.10) | collective-permute-done | bytes 1310752 | tf_op jit(solution)/shard_map/cond/branch_10_fun/ppermute | solution.py:92
  129.5 1.4 copy.110
  131.0 1.4 copy.109
  132.4 0.0 copy-start
  132.4 0.1 slice_negate_fusion
  132.6 0.9 copy-done
  133.5 0.1 slice_negate_fusion.1
  133.7 1.2 maximum_bitcast_fusion.1
  134.9 1.2 maximum_bitcast_fusion
  136.1 2.9 %copy.63 = bf16[2,16,160,128]{3,2,0,1:T(8,128)(2,1)} copy(bf16[2,16,160,128]{2,1,0,3:T(8,128)(2,1)S(1)} %all-to-all-done) | data formatting | bytes 2621440 | tf_op jit(solution)/shard_map/all_to_all | solution.py:87
  138.9 6.7 %bitcast_multiply_fusion = f32[4,16,160,160]{3,2,1,0:T(8,128)} fusion(bf16[1,2,16,160,128]{4,3,1,2,0:T(8,128)(2,1)} %maximum_bitcast_fusion.1, bf16[1,2,16,160,128]{4,3,1,2,0:T(8,128)(2,1)} %bitcast.49, bf16[1,2,16,160,128]{4,3,1,2,0:T(8,128)(2,1)} %maximum_bitcast_fusion, bf16[1,2,16,160,128]{4,3,1,2,0:T(8,128)(2,1)S(1)} %bitcast.48, ...), kind=kOutput, calls=%fused_computation | convolution fusion | flops 848363520 | bytes 13107200 | tf_op jit(solution)/shard_map/qpfiw,qpfjw->qfij/dot_general | solution.py:106
  (4 shorter events, 0.1 us)
Async XLA Ops:
  17.8 2.2 %copy-start.1 = (f32[256,1,8,16]{0,3,1,2:T(8,128)S(1)}, f32[256,1,8,16]{0,3,1,2:T(8,128)}, u32[]{:S(2)}) copy-start(f32[256,1,8,16]{0,3,1,2:T(8,128)} %get-tuple-element.75) | copy-start | bytes 393220
  17.8 2.2 %copy-start.2 = (f32[256,1,8,16]{0,3,1,2:T(8,128)S(1)}, f32[256,1,8,16]{0,3,1,2:T(8,128)}, u32[]{:S(2)}) copy-start(f32[256,1,8,16]{0,3,1,2:T(8,128)} %get-tuple-element.76) | copy-start | bytes 393220
  26.9 10.5 %copy-start.3 = (s32[2,16]{1,0:T(2,128)S(1)}, s32[2,16]{1,0:T(2,128)}, u32[]{:S(2)}) copy-start(s32[2,16]{1,0:T(2,128)} %param.37) | copy-start | bytes 388
  26.9 39.3 %all-to-all-start = ((bf16[2,16,160,128]{2,1,0,3:T(8,128)(2,1)}), bf16[2,16,160,128]{2,1,0,3:T(8,128)(2,1)S(1)}, u32[]{:S(2)}, u32[]{:S(2)}) async-start(bf16[2,16,160,128]{2,1,0,3:T(8,128)(2,1)} %bitcast.47), calls=%async_computation | async-start | bytes 4194304 | tf_op jit(solution)/shard_map/all_to_all | solution.py:87
  68.3 30.4 %collective-permute-start.16 = (bf16[2,16,160,128]{3,2,1,0:T(8,128)(2,1)S(1)}, bf16[2,16,160,128]{3,2,1,0:T(8,128)(2,1)}, u32[]{:S(2)}, u32[]{:S(2)}) collective-permute-start(bf16[2,16,160,128]{3,2,1,0:T(8,128)(2,1)S(1)} %param.16), channel_id=1, source_target_pairs={{0,16},{8,24},{16,0},{24,8},{32,48},{40,56},{48,32},{56,40},{64,80... | collective-permute-start | bytes 3932168 | tf_op jit(solution)/shard_map/cond/branch_1_fun/ppermute | solution.py:92
  98.6 30.9 %collective-permute-start.10 = (bf16[2,16,160,128]{3,2,1,0:T(8,128)(2,1)S(1)}, bf16[2,16,160,128]{3,2,1,0:T(8,128)(2,1)}, u32[]{:S(2)}, u32[]{:S(2)}) collective-permute-start(bf16[2,16,160,128]{3,2,1,0:T(8,128)(2,1)S(1)} %param.10), channel_id=1, source_target_pairs={{0,88},{8,80},{16,72},{24,64},{32,120},{40,112},{48,104},{56,96},{... | collective-permute-start | bytes 3932168 | tf_op jit(solution)/shard_map/cond/branch_10_fun/ppermute | solution.py:92
  132.4 1.1 copy-start

commit v5 on v4

--- a/solution.py
+++ b/solution.py
@@ -42,29 +42,18 @@
 
 def window_spectrum(segment, offset, table, level_matrix, transform, blocks, bands):
     span = table.shape[0]
-    half = W // 2
-    rows = span - half * DEC
-    decimated = jnp.concatenate(
-        [
-            jnp.dot(
-                lax.dynamic_slice_in_dim(segment, offset + start * DEC, rows, 1),
-                table[start * DEC : start * DEC + rows, start : start + half],
-                preferred_element_type=jnp.float32,
-            )
-            for start in (0, half)
-        ],
-        axis=1,
-    )
+    piece = lax.dynamic_slice_in_dim(segment, offset, span, 1)
+    decimated = jnp.dot(piece, table, preferred_element_type=jnp.float32)
     level = jnp.dot(jnp.abs(decimated), level_matrix, precision=lax.Precision.HIGHEST) / (
         2 * HALF + 1
     )
     normed = decimated / (level + 1e-05)
     channels = segment.shape[0]
-    ordered = transform.reshape(W, 2, bands, NF // bands).transpose(0, 2, 1, 3).reshape(W, 2 * NF)
+    ordered = transform.reshape(W, 2, bands, NF // bands).transpose(2, 1, 3, 0).reshape(2 * NF, W)
     spectrum = jnp.einsum(
-        "ain,nk->aki",
+        "akn,ain->aki",
+        jnp.broadcast_to(ordered[None], (blocks, 2 * NF, W)),
         normed.reshape(blocks, channels // blocks, W),
-        ordered,
         precision=lax.Precision.HIGHEST,
     )
     return spectrum.reshape(blocks, bands, 2, NF // bands, channels // blocks).astype(jnp.bfloat16)

time: 148 us -> 140 us (0.946)
  matrix products: 24.6 us -> 20.6 us
  local copies, waits for them, and re-layouts: 16.2 us -> 12.4 us
    div x1 -> x0, local copies, waits for them, and re-layouts: 2.19 us -> none  [window_spectrum(): normed = decimated / (level + 1e-05)]
    dot_general x3 -> x2, matrix products: 13.6 us -> 11.6 us  [the longest x1 7.15 us: window_spectrum(): decimated = jnp.dot(piece, table, preferred_element_type=jnp.float32)]
    dot_general x1, matrix products: 3.41 us -> 1.5 us  [window_spectrum(): jnp.dot(jnp.abs(decimated), level_matrix, precision=lax.Precision.HIGHEST)]
where the time goes in v5:
time: 140 us; the launch traced here: 139 us
  waiting for transfers between devices  86.9 us (62%)
  matrix products  20.6 us (15%)
  local copies, waits for them, and re-layouts  12.4 us (9%)
  starting transfers between devices  11.5 us (8%)
  other arithmetic  4.96 us (4%)
  between operations  2.04 us (1%)
    ppermute x2, waiting for transfers between devices, branch(): return lambda x: lax.ppermute(x, 'chan', pairs)  60 us
    all_to_all x1, waiting for transfers between devices, body(): lax.all_to_all(arranged, ('chan', 'band'), split_axis=3, concat_axis=3, t...  26.9 us
    all_to_all x1, starting transfers between devices, body(): lax.all_to_all(arranged, ('chan', 'band'), split_axis=3, concat_axis=3, t...  10.5 us
    dot_general x1, matrix products, window_spectrum(): decimated = jnp.dot(piece, table, preferred_element_type=jnp.float32)  7.15 us
    dot_general x1, matrix products, body(): jnp.einsum('qpfiw,qpfjw->qfij', own, mixed, preferred_element_type=jnp.fl...  6.74 us
    all_to_all x2, local copies, waits for them, and re-layouts, body(): lax.all_to_all(arranged, ('chan', 'band'), split_axis=3, concat_axis=3, t...  4.88 us
    dot_general x1, matrix products, window_spectrum(): jnp.einsum('akn,ain->aki', jnp.broadcast_to(ordered[None], (blocks, 2 * N...  4.43 us
    convert_element_type x1, local copies, waits for them, and re-layouts, window_spectrum(): spectrum.reshape(blocks, bands, 2, NF // bands, channels // blocks)  2.89 us
  transfers between devices with their start and end apart: 3, of which 3 were waited for; matrix products, arithmetic and copies ran while one was open for 0% of the time, Pallas kernels for 0%

profile of v5, /device:TPU:2, one launch (start us, length us, event | category | flops | bytes accessed | tf_op | source)
XLA Modules:
  0.0 138.5 jit_solution(7946640515616984103)
XLA Ops:
  0.7 0.7 pad.4
  1.4 0.1 reshape.134
  1.4 1.3 fusion.34
  2.7 0.8 convert_bitcast_fusion
  3.6 0.5 convert_element_type.38
  4.0 1.0 pad_maximum_fusion
  5.0 7.1 %fusion = f32[2560,256]{1,0:T(8,128)S(1)} fusion(bf16[2620,256]{1,0:T(8,128)(2,1)S(1)} %convert_element_type.38, bf16[1,2560,2747]{1,2,0:T(8,128)(2,1)} %param.34, s32[]{:T(128)S(6)} %select_n.24), kind=kOutput, calls=%fused_computation | convolution fusion | flops 3434086400 | bytes 17397764 | tf_op jit(solution)/shard_map/dot_general | solution.py:46
  12.2 1.5 %fusion.12 = f32[2560,256]{1,0:T(8,128)S(1)} fusion(f32[2560,256]{1,0:T(8,128)S(1)} %fusion, s32[256]{0:T(256)S(1)} %get-tuple-element.80, s32[256]{0:T(256)S(1)} %get-tuple-element.79), kind=kOutput, calls=%fused_computation.14 | convolution fusion | flops 2016083968 | bytes 5244928 | tf_op jit(solution)/shard_map/dot_general | solution.py:47
  13.7 4.4 %fusion.20 = bf16[16,256,160]{1,2,0:T(8,128)(2,1)S(1)} fusion(f32[16,160,256]{2,1,0:T(8,128)S(1)} %bitcast.40, f32[256,256]{1,0:T(8,128)S(1)} %bitcast.41), kind=kOutput, calls=%fused_computation.22 | convolution fusion | flops 2013921280 | bytes 4194304 | tf_op jit(solution)/shard_map/akn,ain->aki/dot_general | solution.py:53
  18.1 2.9 %copy.52 = bf16[16,256,160]{2,1,0:T(8,128)(2,1)} copy(bf16[16,256,160]{1,2,0:T(8,128)(2,1)S(1)} %fusion.20) | data formatting | bytes 2621440 | tf_op jit(solution)/shard_map/convert_element_type | solution.py:59
  21.0 0.0 copy-start.1
  21.0 10.5 %all-to-all-start = ((bf16[2,16,160,128]{2,1,0,3:T(8,128)(2,1)}), bf16[2,16,160,128]{2,1,0,3:T(8,128)(2,1)S(1)}, u32[]{:S(2)}, u32[]{:S(2)}) async-start(bf16[2,16,160,128]{2,1,0,3:T(8,128)(2,1)} %bitcast.37), calls=%async_computation | async-start | bytes 4194304 | tf_op jit(solution)/shard_map/all_to_all | solution.py:76
  31.5 0.0 copy-done.1
  31.6 0.6 fusion.37
  33.4 26.9 %all-to-all-done = bf16[2,16,160,128]{2,1,0,3:T(8,128)(2,1)S(1)} async-done(((bf16[2,16,160,128]{2,1,0,3:T(8,128)(2,1)}), bf16[2,16,160,128]{2,1,0,3:T(8,128)(2,1)S(1)}, u32[]{:S(2)}, u32[]{:S(2)}) %all-to-all-start) | async-done | bytes 1310752 | tf_op jit(solution)/shard_map/all_to_all | solution.py:76
  60.3 2.0 %copy.56 = bf16[2,16,160,128]{3,2,1,0:T(8,128)(2,1)S(1)} copy(bf16[2,16,160,128]{2,1,0,3:T(8,128)(2,1)S(1)} %all-to-all-done) | data formatting | bytes 2621440 | tf_op jit(solution)/shard_map/all_to_all | solution.py:76
  62.3 31.6 %conditional.3 = (bf16[2,16,160,128]{3,2,1,0:T(8,128)(2,1)}) conditional(s32[]{:T(128)} %bitcast.12, bf16[2,16,160,128]{3,2,1,0:T(8,128)(2,1)S(1)} %copy.56, bf16[2,16,160,128]{3,2,1,0:T(8,128)(2,1)S(1)} %copy.56, bf16[2,16,160,128]{3,2,1,0:T(8,128)(2,1)S(1)} %copy.56, ...), branch_computations={%region_15.16_spmd, %region_16.17_spmd, %region_17.18_spmd, %regio... | conditional | bytes 5242928 | solution.py:84
  62.3 1.0 collective-permute-start.20
  63.4 30.6 %collective-permute-done.20 = bf16[2,16,160,128]{3,2,1,0:T(8,128)(2,1)} collective-permute-done((bf16[2,16,160,128]{3,2,1,0:T(8,128)(2,1)S(1)}, bf16[2,16,160,128]{3,2,1,0:T(8,128)(2,1)}, u32[]{:S(2)}, u32[]{:S(2)}) %collective-permute-start.20) | collective-permute-done | bytes 1310752 | tf_op jit(solution)/shard_map/cond/branch_5_fun/ppermute | solution.py:81
  93.9 29.4 %conditional.2 = (bf16[2,16,160,128]{3,2,1,0:T(8,128)(2,1)}) conditional(s32[]{:T(128)} %bitcast.9, bf16[2,16,160,128]{3,2,1,0:T(8,128)(2,1)S(1)} %copy.56, bf16[2,16,160,128]{3,2,1,0:T(8,128)(2,1)S(1)} %copy.56, bf16[2,16,160,128]{3,2,1,0:T(8,128)(2,1)S(1)} %copy.56, ...), branch_computations={%region_0.1_spmd, %region_1.2_spmd, %region_2.3_spmd, %region_3.4_... | conditional | bytes 5242928 | solution.py:84
  93.9 0.0 collective-permute-start.1
  93.9 29.4 %collective-permute-done.1 = bf16[2,16,160,128]{3,2,1,0:T(8,128)(2,1)} collective-permute-done((bf16[2,16,160,128]{3,2,1,0:T(8,128)(2,1)S(1)}, bf16[2,16,160,128]{3,2,1,0:T(8,128)(2,1)}, u32[]{:S(2)}, u32[]{:S(2)}) %collective-permute-start.1) | collective-permute-done | bytes 1310752 | tf_op jit(solution)/shard_map/cond/branch_1_fun/ppermute | solution.py:81
  123.3 1.4 %copy.99 = bf16[2,16,160,128]{3,2,0,1:T(8,128)(2,1)S(1)} copy(bf16[2,16,160,128]{3,2,1,0:T(8,128)(2,1)} %get-tuple-element.81) | data formatting | bytes 2621440 | tf_op jit(solution)/shard_map/cond | solution.py:84
  124.8 1.4 %copy.98 = bf16[2,16,160,128]{3,2,0,1:T(8,128)(2,1)S(1)} copy(bf16[2,16,160,128]{3,2,1,0:T(8,128)(2,1)} %get-tuple-element.82) | data formatting | bytes 2621440 | tf_op jit(solution)/shard_map/cond | solution.py:84
  126.2 0.0 copy-start
  126.2 0.1 slice_negate_fusion
  126.4 0.1 slice_negate_fusion.1
  126.5 1.2 maximum_bitcast_fusion.1
  127.7 0.0 copy-done
  127.7 1.2 maximum_bitcast_fusion
  128.9 2.9 %copy.55 = bf16[2,16,160,128]{3,2,0,1:T(8,128)(2,1)} copy(bf16[2,16,160,128]{2,1,0,3:T(8,128)(2,1)S(1)} %all-to-all-done) | data formatting | bytes 2621440 | tf_op jit(solution)/shard_map/all_to_all | solution.py:76
  131.8 6.7 %bitcast_multiply_fusion = f32[4,16,160,160]{3,2,1,0:T(8,128)} fusion(bf16[1,2,16,160,128]{4,3,1,2,0:T(8,128)(2,1)} %maximum_bitcast_fusion.1, bf16[1,2,16,160,128]{4,3,1,2,0:T(8,128)(2,1)} %bitcast.39, bf16[1,2,16,160,128]{4,3,1,2,0:T(8,128)(2,1)} %maximum_bitcast_fusion, bf16[1,2,16,160,128]{4,3,1,2,0:T(8,128)(2,1)S(1)} %bitcast.38, ...), kind=kOutput, calls=%fused_computation.3 | convolution fusion | flops 848363520 | bytes 13107200 | tf_op jit(solution)/shard_map/qpfiw,qpfjw->qfij/dot_general | solution.py:95
  (3 shorter events, 0.0 us)
Async XLA Ops:
  21.0 10.5 %copy-start.1 = (s32[2,16]{1,0:T(2,128)S(1)}, s32[2,16]{1,0:T(2,128)}, u32[]{:S(2)}) copy-start(s32[2,16]{1,0:T(2,128)} %param.37) | copy-start | bytes 388
  21.0 39.3 %all-to-all-start = ((bf16[2,16,160,128]{2,1,0,3:T(8,128)(2,1)}), bf16[2,16,160,128]{2,1,0,3:T(8,128)(2,1)S(1)}, u32[]{:S(2)}, u32[]{:S(2)}) async-start(bf16[2,16,160,128]{2,1,0,3:T(8,128)(2,1)} %bitcast.37), calls=%async_computation | async-start | bytes 4194304 | tf_op jit(solution)/shard_map/all_to_all | solution.py:76
  62.3 31.6 %collective-permute-start.20 = (bf16[2,16,160,128]{3,2,1,0:T(8,128)(2,1)S(1)}, bf16[2,16,160,128]{3,2,1,0:T(8,128)(2,1)}, u32[]{:S(2)}, u32[]{:S(2)}) collective-permute-start(bf16[2,16,160,128]{3,2,1,0:T(8,128)(2,1)S(1)} %param.20), channel_id=1, source_target_pairs={{0,48},{8,56},{16,32},{24,40},{32,16},{40,24},{48,0},{56,8},{64,11... | collective-permute-start | bytes 3932168 | tf_op jit(solution)/shard_map/cond/branch_5_fun/ppermute | solution.py:81
  93.9 29.4 %collective-permute-start.1 = (bf16[2,16,160,128]{3,2,1,0:T(8,128)(2,1)S(1)}, bf16[2,16,160,128]{3,2,1,0:T(8,128)(2,1)}, u32[]{:S(2)}, u32[]{:S(2)}) collective-permute-start(bf16[2,16,160,128]{3,2,1,0:T(8,128)(2,1)S(1)} %param.1), channel_id=1, source_target_pairs={{0,16},{8,24},{16,0},{24,8},{32,48},{40,56},{48,32},{56,40},{64,80... | collective-permute-start | bytes 3932168 | tf_op jit(solution)/shard_map/cond/branch_1_fun/ppermute | solution.py:81
  126.2 1.5 %copy-start = (bf16[2,16,160,128]{3,2,0,1:T(8,128)(2,1)}, bf16[2,16,160,128]{3,2,0,1:T(8,128)(2,1)S(1)}, u32[]{:S(2)}) copy-start(bf16[2,16,160,128]{3,2,0,1:T(8,128)(2,1)S(1)} %copy.98) | copy-start | bytes 3932164

commit v6 on v5

--- a/solution.py
+++ b/solution.py
@@ -86,13 +86,11 @@
     first_other = exchange(local, partner[0, 0])
     second_other = exchange(local, partner[1, 0])
     factor = 1.0 / (W * math.sqrt(local.shape[3]))
-    columns = []
-    for other_rows in (first_other, second_other):
-        columns.append(other_rows)
-        columns.append(jnp.stack([-other_rows[1], other_rows[0]]))
-    mixed = jnp.stack(columns)
-    own = jnp.broadcast_to(local[None], mixed.shape)
-    product = jnp.einsum("qpfiw,qpfjw->qfij", own, mixed, preferred_element_type=jnp.float32)
+    variants = jnp.stack([local, jnp.stack([local[1], -local[0]])])
+    rounds = jnp.stack([first_other, second_other])
+    own = jnp.broadcast_to(variants[None], (2,) + variants.shape)
+    mixed = jnp.broadcast_to(rounds[:, None], (2, 2) + rounds.shape[1:])
+    product = jnp.einsum("rqpfiw,rqpfjw->rqfij", own, mixed, preferred_element_type=jnp.float32)
     return (product * factor).reshape(2, 2, bins, width, width)
 
 

time: 140 us -> 145 us (1.036); the launches traced: 139 us -> 145 us
  waiting for transfers between devices: 86.9 us -> 90.3 us
    another operation x0 -> x1, local copies, waits for them, and re-layouts: none -> 6.43 us  [body(): variants = jnp.stack([local, jnp.stack([local[1], -local[0]])])]
    ppermute x2, waiting for transfers between devices: 60 us -> 63.3 us  [branch(): return lambda x: lax.ppermute(x, 'chan', pairs)]
    all_to_all x2 -> x1, local copies, waits for them, and re-layouts: 4.88 us -> 1.98 us  [body(): lax.all_to_all(arranged, ('chan', 'band'), split_axis=3, concat_axis=3, t...]
    cond x2 -> x0, local copies, waits for them, and re-layouts: 2.88 us -> none  [exchange(): return lax.switch(number - 1, branches, rows)]
where the time goes in v6:
time: 145 us
  waiting for transfers between devices  90.3 us (62%)
  matrix products  21.6 us (15%)
  local copies, waits for them, and re-layouts  13 us (9%)
  starting transfers between devices  12.4 us (9%)
  other arithmetic  5.68 us (4%)
  between operations  1.95 us (1%)
    ppermute x2, waiting for transfers between devices, branch(): return lambda x: lax.ppermute(x, 'chan', pairs)  63.3 us
    all_to_all x1, waiting for transfers between devices, body(): lax.all_to_all(arranged, ('chan', 'band'), split_axis=3, concat_axis=3, t...  27.1 us
    all_to_all x1, starting transfers between devices, body(): lax.all_to_all(arranged, ('chan', 'band'), split_axis=3, concat_axis=3, t...  10.5 us
    dot_general x1, matrix products, body(): jnp.einsum('rqpfiw,rqpfjw->rqfij', own, mixed, preferred_element_type=jnp...  7.76 us
    dot_general x1, matrix products, window_spectrum(): decimated = jnp.dot(piece, table, preferred_element_type=jnp.float32)  7.15 us
    another operation x1, local copies, waits for them, and re-layouts, body(): variants = jnp.stack([local, jnp.stack([local[1], -local[0]])])  6.43 us
    dot_general x1, matrix products, window_spectrum(): jnp.einsum('akn,ain->aki', jnp.broadcast_to(ordered[None], (blocks, 2 * N...  4.43 us
    another operation x2, other arithmetic, body(): variants = jnp.stack([local, jnp.stack([local[1], -local[0]])])  3.23 us
  transfers between devices with their start and end apart: 3, of which 3 were waited for; matrix products, arithmetic and copies ran while one was open for 0% of the time, Pallas kernels for 0%

profile of v6, /device:TPU:2, one launch (start us, length us, event | category | flops | bytes accessed | tf_op | source)
XLA Modules:
  0.0 145.0 jit_solution(4420618532952409596)
XLA Ops:
  0.7 0.7 pad.4
  1.4 0.1 reshape.131
  1.4 1.3 fusion.25
  2.7 0.8 convert_bitcast_fusion
  3.5 0.5 convert_element_type.38
  4.0 1.0 pad_maximum_fusion.2
  5.0 7.1 %fusion = f32[2560,256]{1,0:T(8,128)S(1)} fusion(bf16[2620,256]{1,0:T(8,128)(2,1)S(1)} %convert_element_type.38, bf16[1,2560,2747]{1,2,0:T(8,128)(2,1)} %param.34, s32[]{:T(128)S(6)} %select_n.24), kind=kOutput, calls=%fused_computation | convolution fusion | flops 3434086400 | bytes 17397764 | tf_op jit(solution)/shard_map/dot_general | solution.py:46
  12.2 1.5 %fusion.4 = f32[2560,256]{1,0:T(8,128)S(1)} fusion(f32[2560,256]{1,0:T(8,128)S(1)} %fusion, s32[256]{0:T(256)S(1)} %get-tuple-element.76, s32[256]{0:T(256)S(1)} %get-tuple-element.75), kind=kOutput, calls=%fused_computation.7 | convolution fusion | flops 2016083968 | bytes 5244928 | tf_op jit(solution)/shard_map/dot_general | solution.py:47
  13.7 4.4 %fusion.11 = bf16[16,256,160]{1,2,0:T(8,128)(2,1)S(1)} fusion(f32[16,160,256]{2,1,0:T(8,128)S(1)} %bitcast.61, f32[256,256]{1,0:T(8,128)S(1)} %bitcast.62), kind=kOutput, calls=%fused_computation.18 | convolution fusion | flops 2013921280 | bytes 4194304 | tf_op jit(solution)/shard_map/akn,ain->aki/dot_general | solution.py:53
  18.1 2.9 %copy.42 = bf16[16,256,160]{2,1,0:T(8,128)(2,1)} copy(bf16[16,256,160]{1,2,0:T(8,128)(2,1)S(1)} %fusion.11) | data formatting | bytes 2621440 | tf_op jit(solution)/shard_map/convert_element_type | solution.py:59
  21.0 0.0 copy-start
  21.0 10.5 %all-to-all-start = ((bf16[2,16,160,128]{2,1,0,3:T(8,128)(2,1)}), bf16[2,16,160,128]{2,1,0,3:T(8,128)(2,1)S(1)}, u32[]{:S(2)}, u32[]{:S(2)}) async-start(bf16[2,16,160,128]{2,1,0,3:T(8,128)(2,1)} %bitcast.60), calls=%async_computation | async-start | bytes 4194304 | tf_op jit(solution)/shard_map/all_to_all | solution.py:76
  31.5 0.0 copy-done
  31.5 0.5 fusion.28
  33.3 27.1 %all-to-all-done = bf16[2,16,160,128]{2,1,0,3:T(8,128)(2,1)S(1)} async-done(((bf16[2,16,160,128]{2,1,0,3:T(8,128)(2,1)}), bf16[2,16,160,128]{2,1,0,3:T(8,128)(2,1)S(1)}, u32[]{:S(2)}, u32[]{:S(2)}) %all-to-all-start) | async-done | bytes 1310752 | tf_op jit(solution)/shard_map/all_to_all | solution.py:76
  60.3 2.0 %copy.46 = bf16[2,16,160,128]{3,2,1,0:T(8,128)(2,1)S(1)} copy(bf16[2,16,160,128]{2,1,0,3:T(8,128)(2,1)S(1)} %all-to-all-done) | data formatting | bytes 2621440 | tf_op jit(solution)/shard_map/all_to_all | solution.py:76
  62.3 32.5 %conditional.3 = (bf16[1,2,16,160,128]{4,3,2,1,0:T(8,128)(2,1)}) conditional(s32[]{:T(128)} %bitcast.42, bf16[2,16,160,128]{3,2,1,0:T(8,128)(2,1)S(1)} %copy.46, bf16[2,16,160,128]{3,2,1,0:T(8,128)(2,1)S(1)} %copy.46, bf16[2,16,160,128]{3,2,1,0:T(8,128)(2,1)S(1)} %copy.46, ...), branch_computations={%region_15.16_spmd, %region_16.17_spmd, %region_17.18_spmd, %regio... | conditional | bytes 5242928 | solution.py:84
  62.3 0.8 collective-permute-start.19
  63.1 31.7 %collective-permute-done.19 = bf16[2,16,160,128]{3,2,1,0:T(8,128)(2,1)} collective-permute-done((bf16[2,16,160,128]{3,2,1,0:T(8,128)(2,1)S(1)}, bf16[2,16,160,128]{3,2,1,0:T(8,128)(2,1)}, u32[]{:S(2)}, u32[]{:S(2)}) %collective-permute-start.19) | collective-permute-done | bytes 1310752 | tf_op jit(solution)/shard_map/cond/branch_4_fun/ppermute | solution.py:81
  94.8 32.7 %conditional.2 = (bf16[1,2,16,160,128]{4,3,2,1,0:T(8,128)(2,1)}) conditional(s32[]{:T(128)} %bitcast.41, bf16[2,16,160,128]{3,2,1,0:T(8,128)(2,1)S(1)} %copy.46, bf16[2,16,160,128]{3,2,1,0:T(8,128)(2,1)S(1)} %copy.46, bf16[2,16,160,128]{3,2,1,0:T(8,128)(2,1)S(1)} %copy.46, ...), branch_computations={%region_0.1_spmd, %region_1.2_spmd, %region_2.3_spmd, %region_3.4_... | conditional | bytes 5242928 | solution.py:84
  94.8 1.1 collective-permute-start.13
  95.8 31.6 %collective-permute-done.13 = bf16[2,16,160,128]{3,2,1,0:T(8,128)(2,1)} collective-permute-done((bf16[2,16,160,128]{3,2,1,0:T(8,128)(2,1)S(1)}, bf16[2,16,160,128]{3,2,1,0:T(8,128)(2,1)}, u32[]{:S(2)}, u32[]{:S(2)}) %collective-permute-start.13) | collective-permute-done | bytes 1310752 | tf_op jit(solution)/shard_map/cond/branch_13_fun/ppermute | solution.py:81
  127.5 0.1 fusion.27
  127.6 0.3 maximum_bitcast_fusion
  128.0 2.9 %pad_maximum_fusion = bf16[2,2,16,160,128]{3,2,1,4,0:T(8,128)(2,1)} fusion(bf16[1,2,16,160,128]{3,2,1,4,0:T(8,128)(2,1)S(1)} %maximum_bitcast_fusion, bf16[1,2,16,160,128]{3,2,1,4,0:T(8,128)(2,1)S(1)} %bitcast.59), kind=kLoop, calls=%fused_computation.4 | loop fusion | flops 1310720 | bytes 5242880 | tf_op jit(solution)/shard_map/stack | solution.py:89
  130.8 6.4 %copy.45 = bf16[2,2,16,160,128]{4,3,1,2,0:T(8,128)(2,1)S(1)} copy(bf16[2,2,16,160,128]{3,2,1,4,0:T(8,128)(2,1)} %pad_maximum_fusion) | data formatting | bytes 5242880 | tf_op jit(solution)/shard_map/stack | solution.py:89
  137.3 7.8 %bitcast_multiply_fusion = f32[2,2,16,160,160]{4,3,2,1,0:T(8,128)} fusion(bf16[2,2,16,160,128]{4,3,1,2,0:T(8,128)(2,1)S(1)} %copy.45, bf16[1,2,16,160,128]{4,3,2,1,0:T(8,128)(2,1)} %get-tuple-element.78, bf16[1,2,16,160,128]{4,3,2,1,0:T(8,128)(2,1)} %get-tuple-element.77), kind=kOutput, calls=%fused_computation.3 | convolution fusion | flops 841809920 | bytes 11796480 | tf_op jit(solution)/shard_map/rqpfiw,rqpfjw->rqfij/dot_general | solution.py:93
  (3 shorter events, 0.0 us)
Async XLA Ops:
  21.0 10.5 %copy-start = (s32[2,16]{1,0:T(2,128)S(1)}, s32[2,16]{1,0:T(2,128)}, u32[]{:S(2)}) copy-start(s32[2,16]{1,0:T(2,128)} %param.37) | copy-start | bytes 388
  21.0 39.3 %all-to-all-start = ((bf16[2,16,160,128]{2,1,0,3:T(8,128)(2,1)}), bf16[2,16,160,128]{2,1,0,3:T(8,128)(2,1)S(1)}, u32[]{:S(2)}, u32[]{:S(2)}) async-start(bf16[2,16,160,128]{2,1,0,3:T(8,128)(2,1)} %bitcast.60), calls=%async_computation | async-start | bytes 4194304 | tf_op jit(solution)/shard_map/all_to_all | solution.py:76
  62.3 32.4 %collective-permute-start.19 = (bf16[2,16,160,128]{3,2,1,0:T(8,128)(2,1)S(1)}, bf16[2,16,160,128]{3,2,1,0:T(8,128)(2,1)}, u32[]{:S(2)}, u32[]{:S(2)}) collective-permute-start(bf16[2,16,160,128]{3,2,1,0:T(8,128)(2,1)S(1)} %param.19), channel_id=1, source_target_pairs={{0,40},{8,32},{16,56},{24,48},{32,8},{40,0},{48,24},{56,16},{64,10... | collective-permute-start | bytes 3932168 | tf_op jit(solution)/shard_map/cond/branch_4_fun/ppermute | solution.py:81
  94.8 32.7 %collective-permute-start.13 = (bf16[2,16,160,128]{3,2,1,0:T(8,128)(2,1)S(1)}, bf16[2,16,160,128]{3,2,1,0:T(8,128)(2,1)}, u32[]{:S(2)}, u32[]{:S(2)}) collective-permute-start(bf16[2,16,160,128]{3,2,1,0:T(8,128)(2,1)S(1)} %param.13), channel_id=1, source_target_pairs={{0,112},{8,120},{16,96},{24,104},{32,80},{40,88},{48,64},{56,72},{... | collective-permute-start | bytes 3932168 | tf_op jit(solution)/shard_map/cond/branch_13_fun/ppermute | solution.py:81

commit v7 on v5

--- a/solution.py
+++ b/solution.py
@@ -70,10 +70,10 @@
         raw[0], offsets[0], table, level_matrix, transform, chan_count, band_count
     )
     _, _, part_count, bins, width = spectrum.shape
-    arranged = spectrum.transpose(2, 3, 4, 0, 1).reshape(
+    arranged = spectrum.transpose(2, 3, 4, 1, 0).reshape(
         part_count, bins, width, chan_count * band_count
     )
-    local = lax.all_to_all(arranged, ("chan", "band"), split_axis=3, concat_axis=3, tiled=True)
+    local = lax.all_to_all(arranged, ("band", "chan"), split_axis=3, concat_axis=3, tiled=True)
 
     def exchange(rows, number):
         def branch(shift):

time: 140 us -> 118 us (0.84)
  waiting for transfers between devices: 86.9 us -> 62 us
  local copies, waits for them, and re-layouts: 12.4 us -> 15 us
    ppermute x2, waiting for transfers between devices: 60 us -> 33.6 us  [branch(): return lambda x: lax.ppermute(x, 'chan', pairs)]
    reshape x0 -> x1, local copies, waits for them, and re-layouts: none -> 2.51 us  [body(): spectrum.transpose(2, 3, 4, 1, 0)]
    all_to_all x1, waiting for transfers between devices: 26.9 us -> 28.4 us  [body(): lax.all_to_all(arranged, ('band', 'chan'), split_axis=3, concat_axis=3, t...]
where the time goes in v7:
time: 118 us; the launch traced here: 116 us
  waiting for transfers between devices  62 us (53%)
  matrix products  20.6 us (17%)
  local copies, waits for them, and re-layouts  15 us (13%)
  starting transfers between devices  11 us (9%)
  other arithmetic  4.96 us (4%)
  between operations  2.05 us (2%)
    ppermute x2, waiting for transfers between devices, branch(): return lambda x: lax.ppermute(x, 'chan', pairs)  33.6 us
    all_to_all x1, waiting for transfers between devices, body(): lax.all_to_all(arranged, ('band', 'chan'), split_axis=3, concat_axis=3, t...  28.4 us
    all_to_all x1, starting transfers between devices, body(): lax.all_to_all(arranged, ('band', 'chan'), split_axis=3, concat_axis=3, t...  10.5 us
    dot_general x1, matrix products, window_spectrum(): decimated = jnp.dot(piece, table, preferred_element_type=jnp.float32)  7.15 us
    dot_general x1, matrix products, body(): jnp.einsum('qpfiw,qpfjw->qfij', own, mixed, preferred_element_type=jnp.fl...  6.74 us
    all_to_all x2, local copies, waits for them, and re-layouts, body(): lax.all_to_all(arranged, ('band', 'chan'), split_axis=3, concat_axis=3, t...  4.88 us
    dot_general x1, matrix products, window_spectrum(): jnp.einsum('akn,ain->aki', jnp.broadcast_to(ordered[None], (blocks, 2 * N...  4.43 us
    cond x2, local copies, waits for them, and re-layouts, exchange(): return lax.switch(number - 1, branches, rows)  2.88 us
  transfers between devices with their start and end apart: 3, of which 3 were waited for; matrix products, arithmetic and copies ran while one was open for 0% of the time, Pallas kernels for 0%

profile of v7, /device:TPU:2, one launch (start us, length us, event | category | flops | bytes accessed | tf_op | source)
XLA Modules:
  0.0 115.7 jit_solution(863599080316574022)
XLA Ops:
  0.7 0.7 pad.4
  1.4 0.1 reshape.134
  1.4 1.3 %fusion.34 = (f32[256,1,8,16]{0,3,1,2:T(8,128)}, f32[256,1,8,16]{0,3,1,2:T(8,128)}) fusion(s32[8,16]{1,0:T(8,128)S(1)} %multiply_add_fusion), kind=kLoop, calls=%fused_computation.45 | loop fusion | flops 491520 | bytes 262656 | tf_op jit(solution)/shard_map/cos | solution.py:28
  2.7 0.8 convert_bitcast_fusion
  3.6 0.5 convert_element_type.38
  4.0 1.0 pad_maximum_fusion
  5.0 7.1 %fusion = f32[2560,256]{1,0:T(8,128)S(1)} fusion(bf16[2620,256]{1,0:T(8,128)(2,1)S(1)} %convert_element_type.38, bf16[1,2560,2747]{1,2,0:T(8,128)(2,1)} %param.34, s32[]{:T(128)S(6)} %select_n.24), kind=kOutput, calls=%fused_computation | convolution fusion | flops 3434086400 | bytes 17397764 | tf_op jit(solution)/shard_map/dot_general | solution.py:46
  12.2 1.5 %fusion.12 = f32[2560,256]{1,0:T(8,128)S(1)} fusion(f32[2560,256]{1,0:T(8,128)S(1)} %fusion, s32[256]{0:T(256)S(1)} %get-tuple-element.80, s32[256]{0:T(256)S(1)} %get-tuple-element.79), kind=kOutput, calls=%fused_computation.14 | convolution fusion | flops 2016083968 | bytes 5244928 | tf_op jit(solution)/shard_map/dot_general | solution.py:47
  13.7 4.4 %fusion.20 = bf16[16,256,160]{1,2,0:T(8,128)(2,1)S(1)} fusion(f32[16,160,256]{2,1,0:T(8,128)S(1)} %bitcast.40, f32[256,256]{1,0:T(8,128)S(1)} %bitcast.41), kind=kOutput, calls=%fused_computation.22 | convolution fusion | flops 2013921280 | bytes 4194304 | tf_op jit(solution)/shard_map/akn,ain->aki/dot_general | solution.py:53
  18.1 1.8 %copy.52 = bf16[16,256,160]{2,1,0:T(8,128)(2,1)S(1)} copy(bf16[16,256,160]{1,2,0:T(8,128)(2,1)S(1)} %fusion.20) | data formatting | bytes 2621440 | tf_op jit(solution)/shard_map/convert_element_type | solution.py:59
  19.9 1.2 %copy.53 = bf16[2,16,160,8,16]{2,4,3,1,0:T(8,128)(2,1)S(1)} copy(bf16[2,16,160,8,16]{2,1,0,3,4:T(8,128)(2,1)S(1)} %bitcast.36) | data formatting | bytes 2621440 | tf_op jit(solution)/shard_map/transpose | solution.py:73
  21.1 2.5 %copy.54 = bf16[2,16,160,128]{2,1,0,3:T(8,128)(2,1)} copy(bf16[2,16,160,128]{2,3,1,0:T(8,128)(2,1)S(1)} %bitcast.37) | data formatting | bytes 2621440 | tf_op jit(solution)/shard_map/reshape | solution.py:73
  23.6 0.0 copy-start.1
  23.6 10.5 %all-to-all-start = ((bf16[2,16,160,128]{2,1,0,3:T(8,128)(2,1)}), bf16[2,16,160,128]{2,1,0,3:T(8,128)(2,1)S(1)}, u32[]{:S(2)}, u32[]{:S(2)}) async-start(bf16[2,16,160,128]{2,1,0,3:T(8,128)(2,1)} %copy.54), calls=%async_computation | async-start | bytes 4194304 | tf_op jit(solution)/shard_map/all_to_all | solution.py:76
  34.2 0.0 copy-done.1
  34.2 0.6 fusion.37
  36.0 28.4 %all-to-all-done = bf16[2,16,160,128]{2,1,0,3:T(8,128)(2,1)S(1)} async-done(((bf16[2,16,160,128]{2,1,0,3:T(8,128)(2,1)}), bf16[2,16,160,128]{2,1,0,3:T(8,128)(2,1)S(1)}, u32[]{:S(2)}, u32[]{:S(2)}) %all-to-all-start) | async-done | bytes 1310752 | tf_op jit(solution)/shard_map/all_to_all | solution.py:76
  64.4 2.0 %copy.56 = bf16[2,16,160,128]{3,2,1,0:T(8,128)(2,1)S(1)} copy(bf16[2,16,160,128]{2,1,0,3:T(8,128)(2,1)S(1)} %all-to-all-done) | data formatting | bytes 2621440 | tf_op jit(solution)/shard_map/all_to_all | solution.py:76
  66.3 3.3 %conditional.3 = (bf16[2,16,160,128]{3,2,1,0:T(8,128)(2,1)}) conditional(s32[]{:T(128)} %bitcast.12, bf16[2,16,160,128]{3,2,1,0:T(8,128)(2,1)S(1)} %copy.56, bf16[2,16,160,128]{3,2,1,0:T(8,128)(2,1)S(1)} %copy.56, bf16[2,16,160,128]{3,2,1,0:T(8,128)(2,1)S(1)} %copy.56, ...), branch_computations={%region_15.16_spmd, %region_16.17_spmd, %region_17.18_spmd, %regio... | conditional | bytes 5242928 | solution.py:84
  66.4 0.1 collective-permute-start.15
  66.5 3.2 %collective-permute-done.15 = bf16[2,16,160,128]{3,2,1,0:T(8,128)(2,1)} collective-permute-done((bf16[2,16,160,128]{3,2,1,0:T(8,128)(2,1)S(1)}, bf16[2,16,160,128]{3,2,1,0:T(8,128)(2,1)}, u32[]{:S(2)}, u32[]{:S(2)}) %collective-permute-start.15) | collective-permute-done | bytes 1310752 | tf_op jit(solution)/shard_map/cond/branch_0_fun/ppermute | solution.py:81
  69.6 30.9 %conditional.2 = (bf16[2,16,160,128]{3,2,1,0:T(8,128)(2,1)}) conditional(s32[]{:T(128)} %bitcast.9, bf16[2,16,160,128]{3,2,1,0:T(8,128)(2,1)S(1)} %copy.56, bf16[2,16,160,128]{3,2,1,0:T(8,128)(2,1)S(1)} %copy.56, bf16[2,16,160,128]{3,2,1,0:T(8,128)(2,1)S(1)} %copy.56, ...), branch_computations={%region_0.1_spmd, %region_1.2_spmd, %region_2.3_spmd, %region_3.4_... | conditional | bytes 5242928 | solution.py:84
  69.6 0.4 collective-permute-start.8
  70.0 30.5 %collective-permute-done.8 = bf16[2,16,160,128]{3,2,1,0:T(8,128)(2,1)} collective-permute-done((bf16[2,16,160,128]{3,2,1,0:T(8,128)(2,1)S(1)}, bf16[2,16,160,128]{3,2,1,0:T(8,128)(2,1)}, u32[]{:S(2)}, u32[]{:S(2)}) %collective-permute-start.8) | collective-permute-done | bytes 1310752 | tf_op jit(solution)/shard_map/cond/branch_8_fun/ppermute | solution.py:81
  100.5 1.4 %copy.98 = bf16[2,16,160,128]{3,2,0,1:T(8,128)(2,1)S(1)} copy(bf16[2,16,160,128]{3,2,1,0:T(8,128)(2,1)} %get-tuple-element.81) | data formatting | bytes 2621440 | tf_op jit(solution)/shard_map/cond | solution.py:84
  101.9 1.4 %copy.97 = bf16[2,16,160,128]{3,2,0,1:T(8,128)(2,1)S(1)} copy(bf16[2,16,160,128]{3,2,1,0:T(8,128)(2,1)} %get-tuple-element.82) | data formatting | bytes 2621440 | tf_op jit(solution)/shard_map/cond | solution.py:84
  103.4 0.0 copy-start
  103.4 0.1 slice_negate_fusion
  103.5 0.1 slice_negate_fusion.1
  103.7 1.2 %maximum_bitcast_fusion.1 = bf16[1,2,16,160,128]{4,3,1,2,0:T(8,128)(2,1)} fusion(bf16[1,16,160,128]{3,2,0,1:T(8,128)(2,1)S(1)} %get-tuple-element.74, bf16[1,16,160,128]{3,2,0,1:T(8,128)(2,1)S(1)} %get-tuple-element.73), kind=kLoop, calls=%fused_computation.24 | loop fusion | flops 655360 | bytes 2621440 | tf_op jit(solution)/shard_map/stack | solution.py:93
  104.9 0.0 copy-done
  104.9 1.2 %maximum_bitcast_fusion = bf16[1,2,16,160,128]{4,3,1,2,0:T(8,128)(2,1)} fusion(bf16[1,16,160,128]{3,2,0,1:T(8,128)(2,1)S(1)} %get-tuple-element.70, bf16[1,16,160,128]{3,2,0,1:T(8,128)(2,1)S(1)} %get-tuple-element.69), kind=kLoop, calls=%fused_computation.23 | loop fusion | flops 655360 | bytes 2621440 | tf_op jit(solution)/shard_map/stack | solution.py:93
  106.0 2.9 %copy.55 = bf16[2,16,160,128]{3,2,0,1:T(8,128)(2,1)} copy(bf16[2,16,160,128]{2,1,0,3:T(8,128)(2,1)S(1)} %all-to-all-done) | data formatting | bytes 2621440 | tf_op jit(solution)/shard_map/all_to_all | solution.py:76
  108.9 6.7 %bitcast_multiply_fusion = f32[4,16,160,160]{3,2,1,0:T(8,128)} fusion(bf16[1,2,16,160,128]{4,3,1,2,0:T(8,128)(2,1)} %maximum_bitcast_fusion.1, bf16[1,2,16,160,128]{4,3,1,2,0:T(8,128)(2,1)} %bitcast.39, bf16[1,2,16,160,128]{4,3,1,2,0:T(8,128)(2,1)} %maximum_bitcast_fusion, bf16[1,2,16,160,128]{4,3,1,2,0:T(8,128)(2,1)S(1)} %bitcast.38, ...), kind=kOutput, calls=%fused_computation.3 | convolution fusion | flops 848363520 | bytes 13107200 | tf_op jit(solution)/shard_map/qpfiw,qpfjw->qfij/dot_general | solution.py:95
  (3 shorter events, 0.0 us)
Async XLA Ops:
  23.6 10.5 %copy-start.1 = (s32[2,16]{1,0:T(2,128)S(1)}, s32[2,16]{1,0:T(2,128)}, u32[]{:S(2)}) copy-start(s32[2,16]{1,0:T(2,128)} %param.37) | copy-start | bytes 388
  23.6 40.7 %all-to-all-start = ((bf16[2,16,160,128]{2,1,0,3:T(8,128)(2,1)}), bf16[2,16,160,128]{2,1,0,3:T(8,128)(2,1)S(1)}, u32[]{:S(2)}, u32[]{:S(2)}) async-start(bf16[2,16,160,128]{2,1,0,3:T(8,128)(2,1)} %copy.54), calls=%async_computation | async-start | bytes 4194304 | tf_op jit(solution)/shard_map/all_to_all | solution.py:76
  66.4 3.2 %collective-permute-start.15 = (bf16[2,16,160,128]{3,2,1,0:T(8,128)(2,1)S(1)}, bf16[2,16,160,128]{3,2,1,0:T(8,128)(2,1)}, u32[]{:S(2)}, u32[]{:S(2)}) collective-permute-start(bf16[2,16,160,128]{3,2,1,0:T(8,128)(2,1)S(1)} %param.15), channel_id=1, source_target_pairs={{0,8},{8,0},{16,24},{24,16},{32,40},{40,32},{48,56},{56,48},{64,72... | collective-permute-start | bytes 3932168 | tf_op jit(solution)/shard_map/cond/branch_0_fun/ppermute | solution.py:81
  69.6 30.9 %collective-permute-start.8 = (bf16[2,16,160,128]{3,2,1,0:T(8,128)(2,1)S(1)}, bf16[2,16,160,128]{3,2,1,0:T(8,128)(2,1)}, u32[]{:S(2)}, u32[]{:S(2)}) collective-permute-start(bf16[2,16,160,128]{3,2,1,0:T(8,128)(2,1)S(1)} %param.8), channel_id=1, source_target_pairs={{0,72},{8,64},{16,88},{24,80},{32,104},{40,96},{48,120},{56,112},{... | collective-permute-start | bytes 3932168 | tf_op jit(solution)/shard_map/cond/branch_8_fun/ppermute | solution.py:81
  103.4 1.5 %copy-start = (bf16[2,16,160,128]{3,2,0,1:T(8,128)(2,1)}, bf16[2,16,160,128]{3,2,0,1:T(8,128)(2,1)S(1)}, u32[]{:S(2)}) copy-start(bf16[2,16,160,128]{3,2,0,1:T(8,128)(2,1)S(1)} %copy.97) | copy-start | bytes 3932164
